TPU v7x, 256 devices: a whole 4x4x8 slice. The times are simulated.
256 devices in a mesh: wave: 32 (over z, x), tile: 8 (over y, core).
Axes of the slice: x: 4, y: 4, z: 8, core: 2. Of those that a mesh axis runs over, the one named last changes fastest.
Arguments:
- scene: float32 [32, 2048, 1024], P('wave', 'tile'), may hold values from -6 to 6
- bank: float32 [32, 16, 8, 128, 128], P('wave', 'tile'), may hold values from -0.046875 to 0.046875
- psf_index: int32 [16, 8, 4], P('tile'), may hold values from 0 to 127, as said below
- psf_weight: int32 [16, 8, 4], P('tile'), may hold values from 1 to 32768
- response: float32 [3, 32], replicated, may hold values from -1 to 1
Outputs:
- colour: float32 [3, 2048, 1024], P(None, ('tile', 'wave'))
Inputs may be any that keep to these rules, and one draw needn't show every extreme that they name: Entry k of tile (r, c) names the field point (psf_index // 8, psf_index % 8), which lies at most one tile row and at most one tile column from (r, c); entry 0 names (r, c) itself.
All inputs are finite; a program needn't handle non-finite values.
Results may differ from a plain program's by a relative error of at most 0.0001.
Values sent between devices are 32-bit elements; how exact they have to be, the bound alone decides.
No kernel may reach another device: no remote copies, remote signals or barrier semaphores. Data moves between devices by JAX's collectives and lax.ppermute only.
A program may use at most 64 MiB of HBM per device.

v0:
```python
import math

import jax
import jax.numpy as jnp
from jax import lax
from jax.sharding import PartitionSpec as P

highest = lax.Precision.HIGHEST
high = lax.Precision.HIGH


def with_halo(cells, sides, width):
    for axis, dim in sides:
        count = lax.axis_size(axis)
        ends = count - 1
        head = lax.slice_in_dim(cells, 0, width, axis=dim)
        tail = lax.slice_in_dim(cells, cells.shape[dim] - width, cells.shape[dim], axis=dim)
        cells = jnp.concatenate(
            [
                lax.ppermute(tail, axis, [(i, (i + 1) % count) for i in range(ends)]),
                cells,
                lax.ppermute(head, axis, [((i + 1) % count, i) for i in range(ends)]),
            ],
            axis=dim,
        )
    return cells


def from_behind(shard, axis, by):
    size = lax.axis_size(axis)
    pairs = [(i, i + by) for i in range(size) if 0 <= i + by < size]
    return lax.ppermute(shard, axis, pairs)


def angle_table(rows, cols, length):
    products = lax.iota(jnp.int32, rows)[:, None] * lax.iota(jnp.int32, cols)[None, :] % length
    angles = products.astype(jnp.float32) * (2.0 * math.pi / length)
    return jnp.cos(angles), jnp.sin(angles)


def dft_tables(side):
    length = 2 * side
    half = side
    cos_in, sin_in = angle_table(side, half, length)
    alternating = jnp.where(lax.iota(jnp.int32, side) % 2 == 0, 1.0, -1.0).astype(jnp.float32)
    first = jnp.concatenate([cos_in, (-sin_in).at[:, 0].set(alternating)], axis=1)
    cos_top, sin_top = angle_table(side, length, length)
    rows_fwd = jnp.concatenate([cos_top, sin_top], axis=1)
    cos_full, sin_full = angle_table(length, length, length)
    rows_inv = jnp.concatenate([cos_full, sin_full], axis=1)
    cos_out, sin_out = angle_table(half, length, length)
    every = jnp.where(lax.iota(jnp.int32, length) % 2 == 0, 1.0, -1.0).astype(jnp.float32)
    cos_out = (2.0 * cos_out).at[0].set(1.0)
    sin_out = (-2.0 * sin_out).at[0].set(every)
    last = jnp.concatenate([cos_out, sin_out], axis=0) / float(length * length)
    return first, rows_fwd, rows_inv, last


def forward(blocks, first, rows_fwd):
    half = first.shape[1] // 2
    length = rows_fwd.shape[1] // 2
    packed = jnp.einsum("tab,bj->taj", blocks, first, precision=highest)
    both = jnp.einsum("ak,taj->tkj", rows_fwd, packed, precision=highest)
    by_cos, by_sin = both[:, :length], both[:, length:]
    spec_real = by_cos[..., :half] + by_sin[..., half:]
    spec_imag = by_cos[..., half:] - by_sin[..., :half]
    return spec_real, spec_imag


def reverse(values):
    return jnp.roll(jnp.flip(values, axis=-1), 1, axis=-1)


def split_packed(real, imag):
    real_rev, imag_rev = reverse(real), reverse(imag)
    low = (0.5 * (real + real_rev), 0.5 * (imag - imag_rev))
    top = (0.5 * (imag + imag_rev), -0.5 * (real - real_rev))
    return low, top


def times(a, b):
    return (a[0] * b[0] - a[1] * b[1], a[0] * b[1] + a[1] * b[0])


def product(scene_spec, psf_spec):
    prod_real, prod_imag = times(scene_spec, psf_spec)
    scene_low, scene_top = split_packed(scene_spec[0][..., 0], scene_spec[1][..., 0])
    psf_low, psf_top = split_packed(psf_spec[0][..., 0], psf_spec[1][..., 0])
    low = times(scene_low, psf_low)
    top = times(scene_top, psf_top)
    prod_real = prod_real.at[..., 0].set(low[0] - top[1])
    prod_imag = prod_imag.at[..., 0].set(low[1] + top[0])
    return prod_real, prod_imag


def inverse(prod_real, prod_imag, rows_inv, last):
    half = prod_real.shape[-1]
    length = rows_inv.shape[0]
    stacked = jnp.concatenate([prod_real, prod_imag], axis=-1)
    both = jnp.einsum("km,tkj->tmj", rows_inv, stacked, precision=high)
    by_cos, by_sin = both[:, :length], both[:, length:]
    part_real = by_cos[..., :half] - by_sin[..., half:]
    part_imag = by_sin[..., :half] + by_cos[..., half:]
    packed = jnp.concatenate([part_real, part_imag], axis=-1)
    return jnp.einsum("tmj,jn->tmn", packed, last, precision=high)


def blur_wave(scene_plane, extended_plane, mixing, tables):
    first, rows_fwd, rows_inv, last = tables
    slots, tile_cols, side = (
        extended_plane.shape[0] * extended_plane.shape[1],
        extended_plane.shape[1],
        extended_plane.shape[-1],
    )
    tile_rows = extended_plane.shape[0] - 2
    tiles = tile_rows * tile_cols
    width = scene_plane.shape[1]
    margin = side // 2
    psf_set = jnp.dot(mixing, extended_plane.reshape(slots, side * side), precision=highest)
    psf_set = psf_set.reshape(tiles, side, side)
    tile_set = (
        scene_plane.reshape(tile_rows, side, tile_cols, side)
        .transpose(0, 2, 1, 3)
        .reshape(tiles, side, side)
    )
    spec_real, spec_imag = forward(jnp.concatenate([tile_set, psf_set]), first, rows_fwd)
    prod_real, prod_imag = product(
        (spec_real[:tiles], spec_imag[:tiles]), (spec_real[tiles:], spec_imag[tiles:])
    )
    circular = inverse(prod_real, prod_imag, rows_inv, last)
    circular = circular.reshape(tile_rows, tile_cols, 2 * side, 2 * side)
    left_half = jnp.pad(circular[..., :side], ((0, 0), (0, 1), (0, 0), (0, 0)))
    right_half = jnp.pad(circular[..., side:], ((0, 0), (1, 0), (0, 0), (0, 0)))
    columns = (left_half + right_half).transpose(0, 2, 1, 3)
    columns = columns.reshape(tile_rows, 2 * side, (tile_cols + 1) * side)
    columns = columns[:, :, margin : margin + tile_cols * side]
    top_half = jnp.pad(columns[:, :side], ((0, 1), (0, 0), (0, 0)))
    bottom_half = jnp.pad(columns[:, side:], ((1, 0), (0, 0), (0, 0)))
    return (top_half + bottom_half).reshape((tile_rows + 1) * side, width)


def per_device(scene, bank, psf_index, psf_weight, response):
    wave_count, tile_rows, tile_cols, side = (
        bank.shape[0],
        bank.shape[1],
        bank.shape[2],
        bank.shape[3],
    )
    entries = psf_index.shape[-1]
    margin = side // 2
    strip = tile_rows * side
    extended = with_halo(bank, (("tile", 1),), 1)
    first_slot = (lax.axis_index("tile") * tile_rows - 1) * tile_cols
    local_slot = psf_index.reshape(tile_rows * tile_cols, entries) - first_slot
    slot_ids = lax.iota(jnp.int32, (tile_rows + 2) * tile_cols)
    fraction = psf_weight.reshape(tile_rows * tile_cols, entries).astype(jnp.float32) / 65536.0
    mixing = jnp.sum(
        jnp.where(local_slot[:, :, None] == slot_ids[None, None, :], fraction[:, :, None], 0.0),
        axis=1,
    )
    tables = dft_tables(side)

    def one_wave(inputs):
        return blur_wave(inputs[0], inputs[1], mixing, tables)

    summed = lax.map(one_wave, (scene, extended))
    from_above = from_behind(summed[:, strip + margin :], "tile", 1)
    from_below = from_behind(summed[:, :margin], "tile", -1)
    blurred = summed[:, margin : margin + strip]
    blurred = blurred.at[:, :margin].add(from_above)
    blurred = blurred.at[:, strip - margin :].add(from_below)
    groups = lax.axis_size("wave")
    width = blurred.shape[-1]
    pieces = blurred.reshape(wave_count, groups, strip // groups, width)
    gathered = lax.all_to_all(pieces, "wave", 1, 1, tiled=True)
    channels = response.shape[0]
    spectral = response.reshape(channels, groups, wave_count)
    colour = jnp.einsum("csi,isrx->crx", spectral, gathered, precision=highest)
    return colour


def solution(mesh):
    in_specs = (
        P("wave", "tile", None),
        P("wave", "tile", None, None, None),
        P("tile", None, None),
        P("tile", None, None),
        P(),
    )
    out_specs = P(None, ("tile", "wave"), None)
    return jax.shard_map(
        per_device, mesh=mesh, in_specs=in_specs, out_specs=out_specs, check_vma=False
    )
```

profile of v0, /device:TPU:8, one launch (start us, length us, event | category | flops | bytes accessed | tf_op | source)
XLA Modules:
  0.0 126.9 jit_solution(6660239926227504514)
XLA Ops:
  0.0 2.2 %fusion.67 = (f32[1,1,8,128,128]{4,3,2,1,0:T(8,128)}, f32[1,1,8,128,128]{4,3,2,1,0:T(8,128)S(1)}) fusion(f32[1,2,8,128,128]{4,3,2,1,0:T(8,128)} %param.20), kind=kLoop, calls=%fused_computation.129 | loop fusion | bytes 2097152 | tf_op jit(solution)/shard_map/slice | solution.py:17
  2.2 1.9 %collective-permute-start = (f32[1,1,8,128,128]{4,3,2,1,0:T(8,128)}, f32[1,1,8,128,128]{4,3,2,1,0:T(8,128)}, u32[]{:S(2)}, u32[]{:S(2)}) collective-permute-start(f32[1,1,8,128,128]{4,3,2,1,0:T(8,128)} %get-tuple-element.142), channel_id=1, source_target_pairs={{0,1},{1,2},{2,3},{3,4},{4,5},{5,6},{6,7},{8,9},{9,10},{10,11},{11... | collective-permute-start | bytes 1572872 | tf_op jit(solution)/shard_map/ppermute | solution.py:20
  4.1 3.6 %collective-permute-start.1 = (f32[1,1,8,128,128]{4,3,2,1,0:T(8,128)S(1)}, f32[1,1,8,128,128]{4,3,2,1,0:T(8,128)}, u32[]{:S(2)}, u32[]{:S(2)}) collective-permute-start(f32[1,1,8,128,128]{4,3,2,1,0:T(8,128)S(1)} %get-tuple-element.143), channel_id=1, source_target_pairs={{1,0},{2,1},{3,2},{4,3},{5,4},{6,5},{7,6},{9,8},{10,9},{11,10},{12... | collective-permute-start | bytes 1572872 | tf_op jit(solution)/shard_map/ppermute | solution.py:22
  7.8 0.3 sine_negate_fusion
  8.0 0.6 compare_reduce_fusion
  8.7 0.5 broadcast_multiply_fusion.1
  9.2 0.5 broadcast_multiply_fusion
  9.7 0.0 copy-start.8
  9.7 0.2 copy.139
  9.9 0.1 bitcast_bitcast_fusion.1
  10.0 0.4 copy-done.8
  10.4 0.7 slice_select_fusion
  11.1 0.1 sub.70
  11.2 0.1 div.16
  11.3 0.2 copy.113
  11.5 0.6 copy.117
  12.1 0.3 scatter.16
  12.4 0.2 scatter.24
  12.7 0.3 fusion.56
  12.9 0.1 select_reduce_fusion
  13.0 0.5 fusion.48
  13.5 1.7 %fusion.39 = (f32[256,256]{1,0:T(8,128)S(1)}, f32[256,256]{1,0:T(8,128)}) fusion(), kind=kLoop, calls=%fused_computation.63 | loop fusion | flops 917504 | bytes 524288 | tf_op jit(solution)/shard_map/sin | solution.py:38
  15.3 0.0 collective-permute-done
  15.3 1.5 %maximum_bitcast_fusion = f32[4,8,128,128]{3,2,1,0:T(8,128)S(1)} fusion(f32[1,1,8,128,128]{4,3,2,1,0:T(8,128)} %collective-permute-done.1, f32[1,2,8,128,128]{4,3,2,1,0:T(8,128)S(1)} %copy-done.2, f32[1,1,8,128,128]{4,3,2,1,0:T(8,128)} %collective-permute-done), kind=kLoop, calls=%fused_computation.19 | loop fusion | flops 1048576 | bytes 4194304
  16.8 2.2 %fusion.10 = f32[16,128,128]{2,0,1:T(8,128)S(1)} fusion(f32[16,32]{1,0:T(8,128)S(1)} %select_reduce_fusion, f32[4,8,128,128]{3,2,1,0:T(8,128)S(1)} %maximum_bitcast_fusion), kind=kOutput, calls=%fused_computation.14 | convolution fusion | flops 100663296 | bytes 3147776 | tf_op jit(solution)/shard_map/while/body/eval_jaxpr/dot_general | solution.py:119
  19.0 0.3 pad_maximum_fusion.1
  19.3 4.8 %fusion.13 = f32[32,128,256]{1,2,0:T(8,128)S(1)} fusion(f32[32,128,128]{2,0,1:T(8,128)S(1)} %pad_maximum_fusion.1, f32[128,128]{1,0:T(8,128)S(1)} %scatter.16, f32[128,128]{1,0:T(8,128)S(1)} %fusion.56), kind=kOutput, calls=%fused_computation.21 | convolution fusion | flops 1610645504 | bytes 6422528 | tf_op jit(solution)/shard_map/while/body/eval_jaxpr/tab,bj->taj/dot_general | solution.py:62
  24.2 18.7 %convolution_bitcast_fusion = f32[32,512,256]{1,0,2:T(8,128)} fusion(f32[32,128,256]{1,2,0:T(8,128)S(1)} %fusion.13, f32[128,256]{1,0:T(8,128)S(1)} %get-tuple-element.144, f32[128,256]{1,0:T(8,128)S(1)} %get-tuple-element.145), kind=kOutput, calls=%fused_computation | convolution fusion | flops 6442516480 | bytes 21233664 | tf_op jit(solution)/shard_map/while/body/eval_jaxpr/ak,taj->tkj/dot_general | solution.py:63
  42.9 10.3 %slice_add_fusion = (f32[32,256,128]{1,0,2:T(8,128)S(1)}, f32[32,256,128]{1,0,2:T(8,128)}) fusion(f32[32,512,256]{1,0,2:T(8,128)} %convolution_bitcast_fusion), kind=kLoop, calls=%fused_computation.2 | loop fusion | flops 2097152 | bytes 25165824 | tf_op jit(solution)/shard_map/while/body/eval_jaxpr/add | solution.py:65
  53.2 5.7 %multiply_subtract_fusion = (f32[16,256,128]{1,0,2:T(8,128)}, f32[16,256,128]{1,0,2:T(8,128)S(1)}) fusion(f32[32,256,128]{1,0,2:T(8,128)} %get-tuple-element.127, f32[32,256,128]{1,0,2:T(8,128)S(1)} %get-tuple-element.126), kind=kLoop, calls=%fused_computation.24 | loop fusion | flops 3145728 | bytes 12582912 | tf_op jit(solution)/shard_map/while/body/eval_jaxpr/sub | solution.py:82
  58.9 0.7 slice_bitcast_fusion
  59.6 0.1 slice.381
  59.7 0.1 slice.378
  59.8 0.1 slice.375
  59.9 0.1 slice.372
  59.9 0.1 reverse.9
  60.1 0.1 slice_bitcast_fusion.10
  60.2 0.1 reverse.8
  60.3 0.1 slice_bitcast_fusion.11
  60.4 0.1 reverse.11
  60.5 0.1 slice_bitcast_fusion.8
  60.6 0.3 reverse.10
  61.0 0.1 slice_bitcast_fusion.9
  61.0 1.5 %subtract_dynamic-update-slice_fusion = f32[16,256,128]{1,0,2:T(8,128)} fusion(f32[16,256,128]{1,0,2:T(8,128)} %get-tuple-element.130, f32[16,255,1]{1,0,2:T(8,128)S(1)} %slice_bitcast_fusion.11, f32[16,1,1]{1,0,2:T(8,128)S(1)} %slice_bitcast_fusion.7, f32[32,256,128]{1,0,2:T(8,128)} %copy-done.1, f32[16,255,1]{1,0,2:T(8,128)S(1)} %slice_bitcast_fusion.10, ...), kind=kLoop, calls=%fused_computation.97 | loop fusion | flops 110592 | bytes 147456 | tf_op jit(solution)/shard_map/while/body/eval_jaxpr/scatter | solution.py:91
  62.5 0.9 add_dynamic-update-slice_fusion
  63.4 2.2 %pad_maximum_fusion = f32[16,256,256]{1,0,2:T(8,128)S(1)} fusion(f32[16,256,128]{1,0,2:T(8,128)S(1)} %add_dynamic-update-slice_fusion, f32[16,256,128]{1,0,2:T(8,128)} %subtract_dynamic-update-slice_fusion), kind=kLoop, calls=%fused_computation.3 | loop fusion | flops 1048576 | bytes 8388608 | tf_op jit(solution)/shard_map/while/body/eval_jaxpr/concatenate | solution.py:99
  65.5 5.4 %fusion.7 = f32[16,512,256]{1,2,0:T(8,128)S(1)} fusion(f32[16,256,256]{1,0,2:T(8,128)S(1)} %pad_maximum_fusion, f32[256,256]{1,0:T(8,128)S(1)} %get-tuple-element.146, f32[256,256]{1,0:T(8,128)S(1)} %copy-done.3), kind=kOutput, calls=%fused_computation.11 | convolution fusion | flops 3221356544 | bytes 13107200 | tf_op jit(solution)/shard_map/while/body/eval_jaxpr/km,tkj->tmj/dot_general | solution.py:100
  71.0 0.7 slice_subtract_fusion.1
  71.7 0.2 copy-done.6
  71.9 2.1 %fusion = f32[16,256,256]{1,2,0:T(8,128)S(1)} fusion(f32[16,256,128]{1,2,0:T(8,128)S(1)} %get-tuple-element.129, f32[16,256,128]{1,2,0:T(8,128)S(1)} %get-tuple-element.128, f32[128,256]{1,0:T(8,128)S(1)} %scatter.24, f32[128,256]{1,0:T(8,128)S(1)} %copy-done.6), kind=kOutput, calls=%fused_computation.4 | convolution fusion | flops 1611792384 | bytes 8650752 | tf_op jit(solution)/shard_map/while/body/eval_jaxpr/tmj,jn->tmn/dot_general | solution.py:105
  74.0 0.4 fusion.64
  74.5 0.3 pad_add_fusion
  74.7 0.1 fusion.65
  74.9 0.1 pad_add_fusion.1
  75.0 0.5 copy.128
  75.5 3.0 %collective-permute-start.2 = (f32[1,64,1024]{2,1,0:T(8,128)S(1)}, f32[1,64,1024]{2,1,0:T(8,128)S(1)}, u32[]{:S(2)}, u32[]{:S(2)}) collective-permute-start(f32[1,64,1024]{2,1,0:T(8,128)S(1)} %get-tuple-element.141), channel_id=1, source_target_pairs={{0,1},{1,2},{2,3},{3,4},{4,5},{5,6},{6,7},{8,9},{9,10},{10,11},{11... | collective-permute-start | bytes 786440 | tf_op jit(solution)/shard_map/ppermute | solution.py:32
  78.6 2.5 %collective-permute-start.3 = (f32[1,64,1024]{2,1,0:T(8,128)S(1)}, f32[1,64,1024]{2,1,0:T(8,128)S(1)}, u32[]{:S(2)}, u32[]{:S(2)}) collective-permute-start(f32[1,64,1024]{2,1,0:T(8,128)S(1)} %get-tuple-element.140), channel_id=1, source_target_pairs={{1,0},{2,1},{3,2},{4,3},{5,4},{6,5},{7,6},{9,8},{10,9},{11,10},{12... | collective-permute-start | bytes 786440 | tf_op jit(solution)/shard_map/ppermute | solution.py:32
  81.1 0.1 slice.390
  81.2 2.0 %collective-permute-done.2 = f32[1,64,1024]{2,1,0:T(8,128)S(1)} collective-permute-done((f32[1,64,1024]{2,1,0:T(8,128)S(1)}, f32[1,64,1024]{2,1,0:T(8,128)S(1)}, u32[]{:S(2)}, u32[]{:S(2)}) %collective-permute-start.2) | collective-permute-done | bytes 262176 | tf_op jit(solution)/shard_map/ppermute | solution.py:32
  83.3 1.7 %collective-permute-done.3 = f32[1,64,1024]{2,1,0:T(8,128)S(1)} collective-permute-done((f32[1,64,1024]{2,1,0:T(8,128)S(1)}, f32[1,64,1024]{2,1,0:T(8,128)S(1)}, u32[]{:S(2)}, u32[]{:S(2)}) %collective-permute-start.3) | collective-permute-done | bytes 262176 | tf_op jit(solution)/shard_map/ppermute | solution.py:32
  85.0 0.1 fusion.22
  85.1 39.9 %all_to_all.5 = f32[1,32,8,1024]{3,2,0,1:T(8,128)S(1)} all-to-all(f32[1,32,8,1024]{3,2,0,1:T(8,128)S(1)} %bitcast.98), channel_id=1, replica_groups=mesh['wave'=32,'tile'=8] {'wave'}, dimensions={1} | all-to-all | bytes 2097152 | tf_op jit(solution)/shard_map/all_to_all | solution.py:175
  125.0 1.2 convolution_bitcast_fusion.1
  126.2 0.7 copy.131
  (30 shorter events, 0.2 us)
Async XLA Ops:
  0.0 125.0 %copy-start = (f32[3,32]{1,0:T(4,128)S(1)}, f32[3,32]{1,0:T(4,128)}, u32[]{:S(2)}) copy-start(f32[3,32]{1,0:T(4,128)} %param.23) | copy-start | bytes 1156
  0.0 9.7 %copy-start.7 = (s32[2,8,4]{1,2,0:T(4,128)S(1)}, s32[2,8,4]{1,2,0:T(4,128)}, u32[]{:S(2)}) copy-start(s32[2,8,4]{1,2,0:T(4,128)} %param.22) | copy-start | bytes 772
  0.0 9.7 %copy-start.4 = (f32[1,256,1024]{2,1,0:T(8,128)S(1)}, f32[1,256,1024]{2,1,0:T(8,128)}, u32[]{:S(2)}) copy-start(f32[1,256,1024]{2,1,0:T(8,128)} %param.19) | copy-start | bytes 3145732
  2.2 13.1 %collective-permute-start = (f32[1,1,8,128,128]{4,3,2,1,0:T(8,128)}, f32[1,1,8,128,128]{4,3,2,1,0:T(8,128)}, u32[]{:S(2)}, u32[]{:S(2)}) collective-permute-start(f32[1,1,8,128,128]{4,3,2,1,0:T(8,128)} %get-tuple-element.142), channel_id=1, source_target_pairs={{0,1},{1,2},{2,3},{3,4},{4,5},{5,6},{6,7},{8,9},{9,10},{10,11},{11... | collective-permute-start | bytes 1572872 | tf_op jit(solution)/shard_map/ppermute | solution.py:20
  4.1 11.2 %collective-permute-start.1 = (f32[1,1,8,128,128]{4,3,2,1,0:T(8,128)S(1)}, f32[1,1,8,128,128]{4,3,2,1,0:T(8,128)}, u32[]{:S(2)}, u32[]{:S(2)}) collective-permute-start(f32[1,1,8,128,128]{4,3,2,1,0:T(8,128)S(1)} %get-tuple-element.143), channel_id=1, source_target_pairs={{1,0},{2,1},{3,2},{4,3},{5,4},{6,5},{7,6},{9,8},{10,9},{11,10},{12... | collective-permute-start | bytes 1572872 | tf_op jit(solution)/shard_map/ppermute | solution.py:22
  9.7 0.7 copy-start.8
  11.3 4.0 %copy-start.2 = (f32[1,2,8,128,128]{4,3,2,1,0:T(8,128)S(1)}, f32[1,2,8,128,128]{4,3,2,1,0:T(8,128)}, u32[]{:S(2)}) copy-start(f32[1,2,8,128,128]{4,3,2,1,0:T(8,128)} %param.20) | copy-start | bytes 3145732
  12.4 4.3 %copy-start.5 = (f32[128,256]{1,0:T(8,128)}, f32[128,256]{1,0:T(8,128)S(1)}, u32[]{:S(2)}) copy-start(f32[128,256]{1,0:T(8,128)S(1)} %scatter.21) | copy-start | bytes 393220
  53.2 5.7 %copy-start.1 = (f32[32,256,128]{1,0,2:T(8,128)}, f32[32,256,128]{1,0,2:T(8,128)S(1)}, u32[]{:S(2)}) copy-start(f32[32,256,128]{1,0,2:T(8,128)S(1)} %get-tuple-element.126) | copy-start | bytes 12582916
  63.3 2.2 %copy-start.3 = (f32[256,256]{1,0:T(8,128)S(1)}, f32[256,256]{1,0:T(8,128)}, u32[]{:S(2)}) copy-start(f32[256,256]{1,0:T(8,128)} %get-tuple-element.147) | copy-start | bytes 786436
  71.0 0.9 copy-start.6
  75.5 7.7 %collective-permute-start.2 = (f32[1,64,1024]{2,1,0:T(8,128)S(1)}, f32[1,64,1024]{2,1,0:T(8,128)S(1)}, u32[]{:S(2)}, u32[]{:S(2)}) collective-permute-start(f32[1,64,1024]{2,1,0:T(8,128)S(1)} %get-tuple-element.141), channel_id=1, source_target_pairs={{0,1},{1,2},{2,3},{3,4},{4,5},{5,6},{6,7},{8,9},{9,10},{10,11},{11... | collective-permute-start | bytes 786440 | tf_op jit(solution)/shard_map/ppermute | solution.py:32
  78.6 6.4 %collective-permute-start.3 = (f32[1,64,1024]{2,1,0:T(8,128)S(1)}, f32[1,64,1024]{2,1,0:T(8,128)S(1)}, u32[]{:S(2)}, u32[]{:S(2)}) collective-permute-start(f32[1,64,1024]{2,1,0:T(8,128)S(1)} %get-tuple-element.140), channel_id=1, source_target_pairs={{1,0},{2,1},{3,2},{4,3},{5,4},{6,5},{7,6},{9,8},{10,9},{11,10},{12... | collective-permute-start | bytes 786440 | tf_op jit(solution)/shard_map/ppermute | solution.py:32
where the time goes:
time: 129 us; the launch traced here: 127 us
  blocking collectives  39.9 us (31%)
  matrix products  34.6 us (27%)
  other arithmetic  28.6 us (22%)
  starting transfers between devices  11.1 us (9%)
  local copies, waits for them, and re-layouts  8.54 us (7%)
  waiting for transfers between devices  3.76 us (3%)
    all_to_all x1, blocking collectives, per_device(): gathered = lax.all_to_all(pieces, 'wave', 1, 1, tiled=True)  39.9 us
    dot_general x1, matrix products, forward(): both = jnp.einsum('ak,taj->tkj', rows_fwd, packed, precision=highest)  18.7 us
    add x1, other arithmetic, forward(): spec_real = by_cos[..., :half] + by_sin[..., half:]  10.3 us
    sub x1, other arithmetic, times(): return (a[0] * b[0] - a[1] * b[1], a[0] * b[1] + a[1] * b[0])  5.67 us
    ppermute x2, starting transfers between devices, from_behind(): return lax.ppermute(shard, axis, pairs)  5.56 us
    dot_general x1, matrix products, inverse(): both = jnp.einsum('km,tkj->tmj', rows_inv, stacked, precision=high)  5.44 us
    dot_general x1, matrix products, forward(): packed = jnp.einsum('tab,bj->taj', blocks, first, precision=highest)  4.85 us
    ppermute x2, waiting for transfers between devices, from_behind(): return lax.ppermute(shard, axis, pairs)  3.76 us
  transfers between devices with their start and end apart: 4, of which 2 were waited for; matrix products, arithmetic and copies ran while one was open for 6% of the time, Pallas kernels for 0%

commit v1 on v0

--- a/solution.py
+++ b/solution.py
@@ -171,8 +171,14 @@
     blurred = blurred.at[:, strip - margin :].add(from_below)
     groups = lax.axis_size("wave")
     width = blurred.shape[-1]
-    pieces = blurred.reshape(wave_count, groups, strip // groups, width)
-    gathered = lax.all_to_all(pieces, "wave", 1, 1, tiled=True)
+    inner = 4 if groups % 4 == 0 else 1
+    outer = groups // inner
+    pieces = blurred.reshape(wave_count, outer, inner, strip // groups, width)
+    across = [[o * inner + i for i in range(inner)] for o in range(outer)]
+    along = [[o * inner + i for o in range(outer)] for i in range(inner)]
+    pieces = lax.all_to_all(pieces, "wave", 2, 2, tiled=True, axis_index_groups=across)
+    pieces = lax.all_to_all(pieces, "wave", 1, 1, tiled=True, axis_index_groups=along)
+    gathered = pieces.reshape(wave_count, groups, strip // groups, width)
     channels = response.shape[0]
     spectral = response.reshape(channels, groups, wave_count)
     colour = jnp.einsum("csi,isrx->crx", spectral, gathered, precision=highest)

time: 129 us -> 146 us (1.13)
  blocking collectives: 39.9 us -> 57.6 us
    all_to_all x1 -> x2, blocking collectives: 39.9 us -> 57.6 us  [the longest x1 37.6 us: per_device(): lax.all_to_all(pieces, 'wave', 1, 1, tiled=True, axis_index_groups=along)]
  transfers between devices with their start and end apart: 4 -> 4, of which waited for: 2 -> 2; matrix products, arithmetic and copies ran while one was open for 6% -> 5% of each run, Pallas kernels for 0% -> 0%
where the time goes in v1:
time: 146 us; the launch traced here: 145 us
  blocking collectives  57.6 us (39%)
  matrix products  34.6 us (24%)
  other arithmetic  28.6 us (20%)
  starting transfers between devices  11.1 us (8%)
  local copies, waits for them, and re-layouts  8.74 us (6%)
  waiting for transfers between devices  3.76 us (3%)
    all_to_all x1, blocking collectives, per_device(): lax.all_to_all(pieces, 'wave', 1, 1, tiled=True, axis_index_groups=along)  37.6 us
    all_to_all x1, blocking collectives, per_device(): lax.all_to_all(pieces, 'wave', 2, 2, tiled=True, axis_index_groups=across)  20 us
    dot_general x1, matrix products, forward(): both = jnp.einsum('ak,taj->tkj', rows_fwd, packed, precision=highest)  18.7 us
    add x1, other arithmetic, forward(): spec_real = by_cos[..., :half] + by_sin[..., half:]  10.3 us
    sub x1, other arithmetic, times(): return (a[0] * b[0] - a[1] * b[1], a[0] * b[1] + a[1] * b[0])  5.67 us
    ppermute x2, starting transfers between devices, from_behind(): return lax.ppermute(shard, axis, pairs)  5.56 us
    dot_general x1, matrix products, inverse(): both = jnp.einsum('km,tkj->tmj', rows_inv, stacked, precision=high)  5.44 us
    dot_general x1, matrix products, forward(): packed = jnp.einsum('tab,bj->taj', blocks, first, precision=highest)  4.85 us
  transfers between devices with their start and end apart: 4, of which 2 were waited for; matrix products, arithmetic and copies ran while one was open for 5% of the time, Pallas kernels for 0%

profile of v1, /device:TPU:8, one launch (start us, length us, event | category | flops | bytes accessed | tf_op | source)
XLA Modules:
  0.0 144.8 jit_solution(986134112593961371)
XLA Ops:
  0.0 2.2 %fusion.66 = (f32[1,1,8,128,128]{4,3,2,1,0:T(8,128)}, f32[1,1,8,128,128]{4,3,2,1,0:T(8,128)S(1)}) fusion(f32[1,2,8,128,128]{4,3,2,1,0:T(8,128)} %param.20), kind=kLoop, calls=%fused_computation.128 | loop fusion | bytes 2097152 | tf_op jit(solution)/shard_map/slice | solution.py:17
  2.2 1.9 %collective-permute-start = (f32[1,1,8,128,128]{4,3,2,1,0:T(8,128)}, f32[1,1,8,128,128]{4,3,2,1,0:T(8,128)}, u32[]{:S(2)}, u32[]{:S(2)}) collective-permute-start(f32[1,1,8,128,128]{4,3,2,1,0:T(8,128)} %get-tuple-element.142), channel_id=1, source_target_pairs={{0,1},{1,2},{2,3},{3,4},{4,5},{5,6},{6,7},{8,9},{9,10},{10,11},{11... | collective-permute-start | bytes 1572872 | tf_op jit(solution)/shard_map/ppermute | solution.py:20
  4.1 3.6 %collective-permute-start.1 = (f32[1,1,8,128,128]{4,3,2,1,0:T(8,128)S(1)}, f32[1,1,8,128,128]{4,3,2,1,0:T(8,128)}, u32[]{:S(2)}, u32[]{:S(2)}) collective-permute-start(f32[1,1,8,128,128]{4,3,2,1,0:T(8,128)S(1)} %get-tuple-element.143), channel_id=1, source_target_pairs={{1,0},{2,1},{3,2},{4,3},{5,4},{6,5},{7,6},{9,8},{10,9},{11,10},{12... | collective-permute-start | bytes 1572872 | tf_op jit(solution)/shard_map/ppermute | solution.py:22
  7.8 0.3 sine_negate_fusion
  8.0 0.6 compare_reduce_fusion
  8.7 0.5 broadcast_multiply_fusion.1
  9.2 0.5 broadcast_multiply_fusion
  9.7 0.2 copy.143
  9.9 0.1 bitcast_bitcast_fusion.1
  10.0 0.4 copy-done.8
  10.4 0.7 slice_select_fusion
  11.1 0.1 sub.70
  11.2 0.1 div.16
  11.3 0.2 copy.115
  11.5 0.6 copy.119
  12.1 0.3 scatter.16
  12.4 0.2 scatter.24
  12.7 0.3 fusion.55
  12.9 0.1 select_reduce_fusion
  13.0 0.5 fusion.47
  13.5 1.7 %fusion.38 = (f32[256,256]{1,0:T(8,128)S(1)}, f32[256,256]{1,0:T(8,128)}) fusion(), kind=kLoop, calls=%fused_computation.62 | loop fusion | flops 917504 | bytes 524288 | tf_op jit(solution)/shard_map/sin | solution.py:38
  15.3 1.5 %maximum_bitcast_fusion = f32[4,8,128,128]{3,2,1,0:T(8,128)S(1)} fusion(f32[1,1,8,128,128]{4,3,2,1,0:T(8,128)} %collective-permute-done.1, f32[1,2,8,128,128]{4,3,2,1,0:T(8,128)S(1)} %copy-done.2, f32[1,1,8,128,128]{4,3,2,1,0:T(8,128)} %collective-permute-done), kind=kLoop, calls=%fused_computation.19 | loop fusion | flops 1048576 | bytes 4194304
  16.8 2.2 %fusion.10 = f32[16,128,128]{2,0,1:T(8,128)S(1)} fusion(f32[16,32]{1,0:T(8,128)S(1)} %select_reduce_fusion, f32[4,8,128,128]{3,2,1,0:T(8,128)S(1)} %maximum_bitcast_fusion), kind=kOutput, calls=%fused_computation.14 | convolution fusion | flops 100663296 | bytes 3147776 | tf_op jit(solution)/shard_map/while/body/eval_jaxpr/dot_general | solution.py:119
  19.0 0.3 pad_maximum_fusion.1
  19.3 4.8 %fusion.13 = f32[32,128,256]{1,2,0:T(8,128)S(1)} fusion(f32[32,128,128]{2,0,1:T(8,128)S(1)} %pad_maximum_fusion.1, f32[128,128]{1,0:T(8,128)S(1)} %scatter.16, f32[128,128]{1,0:T(8,128)S(1)} %fusion.55), kind=kOutput, calls=%fused_computation.21 | convolution fusion | flops 1610645504 | bytes 6422528 | tf_op jit(solution)/shard_map/while/body/eval_jaxpr/tab,bj->taj/dot_general | solution.py:62
  24.2 18.7 %convolution_bitcast_fusion = f32[32,512,256]{1,0,2:T(8,128)} fusion(f32[32,128,256]{1,2,0:T(8,128)S(1)} %fusion.13, f32[128,256]{1,0:T(8,128)S(1)} %get-tuple-element.144, f32[128,256]{1,0:T(8,128)S(1)} %get-tuple-element.145), kind=kOutput, calls=%fused_computation | convolution fusion | flops 6442516480 | bytes 21233664 | tf_op jit(solution)/shard_map/while/body/eval_jaxpr/ak,taj->tkj/dot_general | solution.py:63
  42.9 10.3 %slice_add_fusion = (f32[32,256,128]{1,0,2:T(8,128)S(1)}, f32[32,256,128]{1,0,2:T(8,128)}) fusion(f32[32,512,256]{1,0,2:T(8,128)} %convolution_bitcast_fusion), kind=kLoop, calls=%fused_computation.2 | loop fusion | flops 2097152 | bytes 25165824 | tf_op jit(solution)/shard_map/while/body/eval_jaxpr/add | solution.py:65
  53.2 5.7 %multiply_subtract_fusion = (f32[16,256,128]{1,0,2:T(8,128)}, f32[16,256,128]{1,0,2:T(8,128)S(1)}) fusion(f32[32,256,128]{1,0,2:T(8,128)} %get-tuple-element.127, f32[32,256,128]{1,0,2:T(8,128)S(1)} %get-tuple-element.126), kind=kLoop, calls=%fused_computation.24 | loop fusion | flops 3145728 | bytes 12582912 | tf_op jit(solution)/shard_map/while/body/eval_jaxpr/sub | solution.py:82
  58.9 0.7 slice_bitcast_fusion
  59.6 0.1 slice.381
  59.7 0.1 slice.378
  59.8 0.1 slice.375
  59.9 0.1 slice.372
  59.9 0.1 reverse.9
  60.1 0.1 slice_bitcast_fusion.10
  60.2 0.1 reverse.8
  60.3 0.1 slice_bitcast_fusion.11
  60.4 0.1 reverse.11
  60.5 0.1 slice_bitcast_fusion.8
  60.6 0.3 reverse.10
  61.0 0.1 slice_bitcast_fusion.9
  61.0 1.5 %subtract_dynamic-update-slice_fusion = f32[16,256,128]{1,0,2:T(8,128)} fusion(f32[16,256,128]{1,0,2:T(8,128)} %get-tuple-element.130, f32[16,255,1]{1,0,2:T(8,128)S(1)} %slice_bitcast_fusion.11, f32[16,1,1]{1,0,2:T(8,128)S(1)} %slice_bitcast_fusion.7, f32[32,256,128]{1,0,2:T(8,128)} %copy-done.1, f32[16,255,1]{1,0,2:T(8,128)S(1)} %slice_bitcast_fusion.10, ...), kind=kLoop, calls=%fused_computation.96 | loop fusion | flops 110592 | bytes 147456 | tf_op jit(solution)/shard_map/while/body/eval_jaxpr/scatter | solution.py:91
  62.5 0.9 add_dynamic-update-slice_fusion
  63.4 2.2 %pad_maximum_fusion = f32[16,256,256]{1,0,2:T(8,128)S(1)} fusion(f32[16,256,128]{1,0,2:T(8,128)S(1)} %add_dynamic-update-slice_fusion, f32[16,256,128]{1,0,2:T(8,128)} %subtract_dynamic-update-slice_fusion), kind=kLoop, calls=%fused_computation.3 | loop fusion | flops 1048576 | bytes 8388608 | tf_op jit(solution)/shard_map/while/body/eval_jaxpr/concatenate | solution.py:99
  65.5 5.4 %fusion.7 = f32[16,512,256]{1,2,0:T(8,128)S(1)} fusion(f32[16,256,256]{1,0,2:T(8,128)S(1)} %pad_maximum_fusion, f32[256,256]{1,0:T(8,128)S(1)} %get-tuple-element.146, f32[256,256]{1,0:T(8,128)S(1)} %copy-done.3), kind=kOutput, calls=%fused_computation.11 | convolution fusion | flops 3221356544 | bytes 13107200 | tf_op jit(solution)/shard_map/while/body/eval_jaxpr/km,tkj->tmj/dot_general | solution.py:100
  71.0 0.7 slice_subtract_fusion.1
  71.7 0.2 copy-done.6
  71.9 2.1 %fusion = f32[16,256,256]{1,2,0:T(8,128)S(1)} fusion(f32[16,256,128]{1,2,0:T(8,128)S(1)} %get-tuple-element.129, f32[16,256,128]{1,2,0:T(8,128)S(1)} %get-tuple-element.128, f32[128,256]{1,0:T(8,128)S(1)} %scatter.24, f32[128,256]{1,0:T(8,128)S(1)} %copy-done.6), kind=kOutput, calls=%fused_computation.4 | convolution fusion | flops 1611792384 | bytes 8650752 | tf_op jit(solution)/shard_map/while/body/eval_jaxpr/tmj,jn->tmn/dot_general | solution.py:105
  74.0 0.4 fusion.63
  74.5 0.3 pad_add_fusion
  74.7 0.1 fusion.64
  74.9 0.1 pad_add_fusion.1
  75.0 0.5 copy.130
  75.5 3.0 %collective-permute-start.2 = (f32[1,64,1024]{2,1,0:T(8,128)S(1)}, f32[1,64,1024]{2,1,0:T(8,128)S(1)}, u32[]{:S(2)}, u32[]{:S(2)}) collective-permute-start(f32[1,64,1024]{2,1,0:T(8,128)S(1)} %get-tuple-element.141), channel_id=1, source_target_pairs={{0,1},{1,2},{2,3},{3,4},{4,5},{5,6},{6,7},{8,9},{9,10},{10,11},{11... | collective-permute-start | bytes 786440 | tf_op jit(solution)/shard_map/ppermute | solution.py:32
  78.6 2.5 %collective-permute-start.3 = (f32[1,64,1024]{2,1,0:T(8,128)S(1)}, f32[1,64,1024]{2,1,0:T(8,128)S(1)}, u32[]{:S(2)}, u32[]{:S(2)}) collective-permute-start(f32[1,64,1024]{2,1,0:T(8,128)S(1)} %get-tuple-element.140), channel_id=1, source_target_pairs={{1,0},{2,1},{3,2},{4,3},{5,4},{6,5},{7,6},{9,8},{10,9},{11,10},{12... | collective-permute-start | bytes 786440 | tf_op jit(solution)/shard_map/ppermute | solution.py:32
  81.1 0.1 slice.390
  81.2 2.0 %collective-permute-done.2 = f32[1,64,1024]{2,1,0:T(8,128)S(1)} collective-permute-done((f32[1,64,1024]{2,1,0:T(8,128)S(1)}, f32[1,64,1024]{2,1,0:T(8,128)S(1)}, u32[]{:S(2)}, u32[]{:S(2)}) %collective-permute-start.2) | collective-permute-done | bytes 262176 | tf_op jit(solution)/shard_map/ppermute | solution.py:32
  83.3 1.7 %collective-permute-done.3 = f32[1,64,1024]{2,1,0:T(8,128)S(1)} collective-permute-done((f32[1,64,1024]{2,1,0:T(8,128)S(1)}, f32[1,64,1024]{2,1,0:T(8,128)S(1)}, u32[]{:S(2)}, u32[]{:S(2)}) %collective-permute-start.3) | collective-permute-done | bytes 262176 | tf_op jit(solution)/shard_map/ppermute | solution.py:32
  85.1 0.1 copy.131
  85.2 20.0 %all_to_all.10 = f32[1,8,4,8,1024]{4,3,1,0,2:T(8,128)S(1)} all-to-all(f32[1,8,4,8,1024]{4,3,1,0,2:T(8,128)S(1)} %copy.131), channel_id=1, replica_groups={{0,8,16,24},{32,40,48,56},{64,72,80,88},{96,104,112,120},{128,136,144,1..., dimensions={2} | all-to-all | bytes 2097152 | tf_op jit(solution)/shard_map/all_to_all | solution.py:179
  105.1 0.1 copy.132
  105.3 37.6 %all_to_all.11 = f32[1,8,4,8,1024]{4,3,2,0,1:T(8,128)S(1)} all-to-all(f32[1,8,4,8,1024]{4,3,2,0,1:T(8,128)S(1)} %copy.132), channel_id=1, replica_groups={{0,32,64,96,128,160,192,224},{8,40,72,104,136,168,200,232},{16,48,80,11..., dimensions={1} | all-to-all | bytes 2097152 | tf_op jit(solution)/shard_map/all_to_all | solution.py:180
  142.8 1.2 convolution_bitcast_fusion.1
  144.1 0.7 copy.134
  (33 shorter events, 0.2 us)
Async XLA Ops:
  0.0 142.8 %copy-start = (f32[3,32]{1,0:T(4,128)S(1)}, f32[3,32]{1,0:T(4,128)}, u32[]{:S(2)}) copy-start(f32[3,32]{1,0:T(4,128)} %param.23) | copy-start | bytes 1156
  0.0 9.7 %copy-start.7 = (s32[2,8,4]{1,2,0:T(4,128)S(1)}, s32[2,8,4]{1,2,0:T(4,128)}, u32[]{:S(2)}) copy-start(s32[2,8,4]{1,2,0:T(4,128)} %param.22) | copy-start | bytes 772
  0.0 9.7 %copy-start.4 = (f32[1,256,1024]{2,1,0:T(8,128)S(1)}, f32[1,256,1024]{2,1,0:T(8,128)}, u32[]{:S(2)}) copy-start(f32[1,256,1024]{2,1,0:T(8,128)} %param.19) | copy-start | bytes 3145732
  2.2 13.1 %collective-permute-start = (f32[1,1,8,128,128]{4,3,2,1,0:T(8,128)}, f32[1,1,8,128,128]{4,3,2,1,0:T(8,128)}, u32[]{:S(2)}, u32[]{:S(2)}) collective-permute-start(f32[1,1,8,128,128]{4,3,2,1,0:T(8,128)} %get-tuple-element.142), channel_id=1, source_target_pairs={{0,1},{1,2},{2,3},{3,4},{4,5},{5,6},{6,7},{8,9},{9,10},{10,11},{11... | collective-permute-start | bytes 1572872 | tf_op jit(solution)/shard_map/ppermute | solution.py:20
  4.1 11.2 %collective-permute-start.1 = (f32[1,1,8,128,128]{4,3,2,1,0:T(8,128)S(1)}, f32[1,1,8,128,128]{4,3,2,1,0:T(8,128)}, u32[]{:S(2)}, u32[]{:S(2)}) collective-permute-start(f32[1,1,8,128,128]{4,3,2,1,0:T(8,128)S(1)} %get-tuple-element.143), channel_id=1, source_target_pairs={{1,0},{2,1},{3,2},{4,3},{5,4},{6,5},{7,6},{9,8},{10,9},{11,10},{12... | collective-permute-start | bytes 1572872 | tf_op jit(solution)/shard_map/ppermute | solution.py:22
  9.7 0.7 copy-start.8
  11.3 4.0 %copy-start.2 = (f32[1,2,8,128,128]{4,3,2,1,0:T(8,128)S(1)}, f32[1,2,8,128,128]{4,3,2,1,0:T(8,128)}, u32[]{:S(2)}) copy-start(f32[1,2,8,128,128]{4,3,2,1,0:T(8,128)} %param.20) | copy-start | bytes 3145732
  12.4 4.3 %copy-start.5 = (f32[128,256]{1,0:T(8,128)}, f32[128,256]{1,0:T(8,128)S(1)}, u32[]{:S(2)}) copy-start(f32[128,256]{1,0:T(8,128)S(1)} %scatter.21) | copy-start | bytes 393220
  53.2 5.7 %copy-start.1 = (f32[32,256,128]{1,0,2:T(8,128)}, f32[32,256,128]{1,0,2:T(8,128)S(1)}, u32[]{:S(2)}) copy-start(f32[32,256,128]{1,0,2:T(8,128)S(1)} %get-tuple-element.126) | copy-start | bytes 12582916
  63.3 2.2 %copy-start.3 = (f32[256,256]{1,0:T(8,128)S(1)}, f32[256,256]{1,0:T(8,128)}, u32[]{:S(2)}) copy-start(f32[256,256]{1,0:T(8,128)} %get-tuple-element.147) | copy-start | bytes 786436
  71.0 0.9 copy-start.6
  75.5 7.7 %collective-permute-start.2 = (f32[1,64,1024]{2,1,0:T(8,128)S(1)}, f32[1,64,1024]{2,1,0:T(8,128)S(1)}, u32[]{:S(2)}, u32[]{:S(2)}) collective-permute-start(f32[1,64,1024]{2,1,0:T(8,128)S(1)} %get-tuple-element.141), channel_id=1, source_target_pairs={{0,1},{1,2},{2,3},{3,4},{4,5},{5,6},{6,7},{8,9},{9,10},{10,11},{11... | collective-permute-start | bytes 786440 | tf_op jit(solution)/shard_map/ppermute | solution.py:32
  78.6 6.4 %collective-permute-start.3 = (f32[1,64,1024]{2,1,0:T(8,128)S(1)}, f32[1,64,1024]{2,1,0:T(8,128)S(1)}, u32[]{:S(2)}, u32[]{:S(2)}) collective-permute-start(f32[1,64,1024]{2,1,0:T(8,128)S(1)} %get-tuple-element.140), channel_id=1, source_target_pairs={{1,0},{2,1},{3,2},{4,3},{5,4},{6,5},{7,6},{9,8},{10,9},{11,10},{12... | collective-permute-start | bytes 786440 | tf_op jit(solution)/shard_map/ppermute | solution.py:32

commit v2 on v0

--- a/solution.py
+++ b/solution.py
@@ -43,28 +43,39 @@
     half = side
     cos_in, sin_in = angle_table(side, half, length)
     alternating = jnp.where(lax.iota(jnp.int32, side) % 2 == 0, 1.0, -1.0).astype(jnp.float32)
-    first = jnp.concatenate([cos_in, (-sin_in).at[:, 0].set(alternating)], axis=1)
+    first = jnp.stack([cos_in, (-sin_in).at[:, 0].set(alternating)], axis=1)
     cos_top, sin_top = angle_table(side, length, length)
-    rows_fwd = jnp.concatenate([cos_top, sin_top], axis=1)
+    rows_fwd = jnp.concatenate(
+        [
+            jnp.concatenate([cos_top.T, sin_top.T], axis=1),
+            jnp.concatenate([-sin_top.T, cos_top.T], axis=1),
+        ],
+        axis=0,
+    )
     cos_full, sin_full = angle_table(length, length, length)
-    rows_inv = jnp.concatenate([cos_full, sin_full], axis=1)
+    rows_inv = jnp.concatenate(
+        [
+            jnp.concatenate([cos_full, -sin_full], axis=1),
+            jnp.concatenate([sin_full, cos_full], axis=1),
+        ],
+        axis=0,
+    )
     cos_out, sin_out = angle_table(half, length, length)
     every = jnp.where(lax.iota(jnp.int32, length) % 2 == 0, 1.0, -1.0).astype(jnp.float32)
     cos_out = (2.0 * cos_out).at[0].set(1.0)
     sin_out = (-2.0 * sin_out).at[0].set(every)
-    last = jnp.concatenate([cos_out, sin_out], axis=0) / float(length * length)
+    last = jnp.stack([cos_out, sin_out], axis=0) / float(length * length)
     return first, rows_fwd, rows_inv, last
 
 
 def forward(blocks, first, rows_fwd):
-    half = first.shape[1] // 2
-    length = rows_fwd.shape[1] // 2
-    packed = jnp.einsum("tab,bj->taj", blocks, first, precision=highest)
-    both = jnp.einsum("ak,taj->tkj", rows_fwd, packed, precision=highest)
-    by_cos, by_sin = both[:, :length], both[:, length:]
-    spec_real = by_cos[..., :half] + by_sin[..., half:]
-    spec_imag = by_cos[..., half:] - by_sin[..., :half]
-    return spec_real, spec_imag
+    tiles, side = blocks.shape[0], blocks.shape[1]
+    half = first.shape[-1]
+    length = rows_fwd.shape[0] // 2
+    packed = jnp.einsum("tab,bpl->tpal", blocks, first, precision=highest)
+    packed = packed.reshape(tiles, 2 * side, half)
+    spec = jnp.einsum("oq,tql->tol", rows_fwd, packed, precision=highest)
+    return spec[:, :length], spec[:, length:]
 
 
 def reverse(values):
@@ -88,21 +99,18 @@
     psf_low, psf_top = split_packed(psf_spec[0][..., 0], psf_spec[1][..., 0])
     low = times(scene_low, psf_low)
     top = times(scene_top, psf_top)
-    prod_real = prod_real.at[..., 0].set(low[0] - top[1])
-    prod_imag = prod_imag.at[..., 0].set(low[1] + top[0])
+    first_column = lax.iota(jnp.int32, prod_real.shape[-1]) == 0
+    prod_real = jnp.where(first_column, (low[0] - top[1])[..., None], prod_real)
+    prod_imag = jnp.where(first_column, (low[1] + top[0])[..., None], prod_imag)
     return prod_real, prod_imag
 
 
 def inverse(prod_real, prod_imag, rows_inv, last):
-    half = prod_real.shape[-1]
-    length = rows_inv.shape[0]
-    stacked = jnp.concatenate([prod_real, prod_imag], axis=-1)
-    both = jnp.einsum("km,tkj->tmj", rows_inv, stacked, precision=high)
-    by_cos, by_sin = both[:, :length], both[:, length:]
-    part_real = by_cos[..., :half] - by_sin[..., half:]
-    part_imag = by_sin[..., :half] + by_cos[..., half:]
-    packed = jnp.concatenate([part_real, part_imag], axis=-1)
-    return jnp.einsum("tmj,jn->tmn", packed, last, precision=high)
+    tiles, length, half = prod_real.shape
+    stacked = jnp.concatenate([prod_real, prod_imag], axis=1)
+    both = jnp.einsum("oq,tql->tol", rows_inv, stacked, precision=high)
+    both = both.reshape(tiles, 2, length, half)
+    return jnp.einsum("tpml,pln->tmn", both, last, precision=high)
 
 
 def blur_wave(scene_plane, extended_plane, mixing, tables):

time: 129 us -> 135 us (1.047)
  local copies, waits for them, and re-layouts: 8.54 us -> 33.5 us
  other arithmetic: 28.6 us -> 15.9 us
  matrix products: 34.6 us -> 29.1 us
    reshape x0 -> x2, local copies, waits for them, and re-layouts: none -> 11.4 us  [the longest x1 5.87 us: inverse(): both = both.reshape(tiles, 2, length, half)]
    add x1 -> x0, other arithmetic: 10.3 us -> none  [forward(): spec_real = by_cos[..., :half] + by_sin[..., half:]]
    dot_general x0 -> x1, local copies, waits for them, and re-layouts: none -> 7.26 us  [inverse(): return jnp.einsum('tpml,pln->tmn', both, last, precision=high)]
    sub x2 -> x0, other arithmetic: 6.38 us -> none  [the longest x1 5.67 us: times(): return (a[0] * b[0] - a[1] * b[1], a[0] * b[1] + a[1] * b[0])]
    dot_general x4, matrix products: 31.1 us -> 25.6 us  [the longest x1 9.81 us: forward(): spec = jnp.einsum('oq,tql->tol', rows_fwd, packed, precision=highest)]
    select_n x0 -> x1, other arithmetic: none -> 4.01 us  [product(): prod_real = jnp.where(first_column, (low[0] - top[1])[..., None], prod_real)]
    unnamed x23 -> x21, local copies, waits for them, and re-layouts: 1.57 us -> 5.2 us
    scatter x2 -> x0, other arithmetic: 2.32 us -> none  [the longest x1 1.46 us: product(): prod_real = prod_real.at[..., 0].set(low[0] - top[1])]
  transfers between devices with their start and end apart: 4 -> 4, of which waited for: 2 -> 2; matrix products, arithmetic and copies ran while one was open for 6% -> 8% of each run, Pallas kernels for 0% -> 0%
where the time goes in v2:
time: 135 us; the launch traced here: 134 us
  blocking collectives  40 us (30%)
  local copies, waits for them, and re-layouts  33.5 us (25%)
  matrix products  29.1 us (22%)
  other arithmetic  15.9 us (12%)
  starting transfers between devices  11.1 us (8%)
  waiting for transfers between devices  3.75 us (3%)
    all_to_all x1, blocking collectives, per_device(): gathered = lax.all_to_all(pieces, 'wave', 1, 1, tiled=True)  40 us
    dot_general x1, matrix products, forward(): spec = jnp.einsum('oq,tql->tol', rows_fwd, packed, precision=highest)  9.81 us
    dot_general x1, local copies, waits for them, and re-layouts, inverse(): return jnp.einsum('tpml,pln->tmn', both, last, precision=high)  7.26 us
    dot_general x1, matrix products, inverse(): both = jnp.einsum('oq,tql->tol', rows_inv, stacked, precision=high)  6.36 us
    reshape x1, local copies, waits for them, and re-layouts, inverse(): both = both.reshape(tiles, 2, length, half)  5.87 us
    ppermute x2, starting transfers between devices, from_behind(): return lax.ppermute(shard, axis, pairs)  5.56 us
    reshape x1, local copies, waits for them, and re-layouts, forward(): packed = packed.reshape(tiles, 2 * side, half)  5.49 us
    dot_general x1, matrix products, forward(): packed = jnp.einsum('tab,bpl->tpal', blocks, first, precision=highest)  5.35 us
  transfers between devices with their start and end apart: 4, of which 2 were waited for; matrix products, arithmetic and copies ran while one was open for 8% of the time, Pallas kernels for 0%

profile of v2, /device:TPU:8, one launch (start us, length us, event | category | flops | bytes accessed | tf_op | source)
XLA Modules:
  0.0 133.7 jit_solution(2908808258136797567)
XLA Ops:
  0.0 2.4 %fusion.82 = (f32[1,1,8,128,128]{4,3,2,1,0:T(8,128)}, f32[1,1,8,128,128]{4,3,2,1,0:T(8,128)}) fusion(f32[1,2,8,128,128]{4,3,2,1,0:T(8,128)} %param.16), kind=kLoop, calls=%fused_computation.151 | loop fusion | bytes 2097152 | tf_op jit(solution)/shard_map/slice | solution.py:17
  2.4 1.9 %collective-permute-start = (f32[1,1,8,128,128]{4,3,2,1,0:T(8,128)}, f32[1,1,8,128,128]{4,3,2,1,0:T(8,128)}, u32[]{:S(2)}, u32[]{:S(2)}) collective-permute-start(f32[1,1,8,128,128]{4,3,2,1,0:T(8,128)} %get-tuple-element.104), channel_id=1, source_target_pairs={{0,1},{1,2},{2,3},{3,4},{4,5},{5,6},{6,7},{8,9},{9,10},{10,11},{11... | collective-permute-start | bytes 1572872 | tf_op jit(solution)/shard_map/ppermute | solution.py:20
  4.3 3.6 %collective-permute-start.1 = (f32[1,1,8,128,128]{4,3,2,1,0:T(8,128)}, f32[1,1,8,128,128]{4,3,2,1,0:T(8,128)}, u32[]{:S(2)}, u32[]{:S(2)}) collective-permute-start(f32[1,1,8,128,128]{4,3,2,1,0:T(8,128)} %get-tuple-element.105), channel_id=1, source_target_pairs={{1,0},{2,1},{3,2},{4,3},{5,4},{6,5},{7,6},{9,8},{10,9},{11,10},{12... | collective-permute-start | bytes 1572872 | tf_op jit(solution)/shard_map/ppermute | solution.py:22
  8.0 0.6 compare_reduce_fusion
  8.7 0.9 sine_negate_fusion
  9.6 0.9 fusion.69
  10.5 0.5 fusion.63
  11.0 0.5 fusion.68
  11.5 0.5 cosine_multiply_fusion
  12.0 0.5 sine_multiply_fusion
  12.6 0.1 sub.62
  12.7 0.1 div.16
  12.8 0.1 select_reduce_fusion
  12.8 0.6 fusion.73
  13.5 0.2 copy.136
  13.7 0.1 copy.107
  13.8 1.5 %scatter.10 = f32[128,1,128]{2,0,1:T(8,128)} dynamic-update-slice(f32[128,1,128]{2,0,1:T(8,128)} %sine_negate_fusion, f32[128,1,1]{2,0,1:T(8,128)S(1)} %copy.107, s32[]{:T(128)} %constant.227.clone.1, s32[]{:T(128)} %constant.227.clone.1, s32[]{:T(128)} %constant.227.clone.1) | dynamic-update-slice | bytes 1028 | tf_op jit(solution)/shard_map/scatter | solution.py:46
  15.4 0.5 scatter.11
  15.9 0.7 scatter.14
  16.5 1.0 fusion.58
  17.5 1.0 fusion.50
  18.5 0.1 copy_bitcast_fusion
  18.7 1.5 %maximum_bitcast_fusion = f32[4,8,128,128]{3,2,1,0:T(8,128)S(1)} fusion(f32[1,1,8,128,128]{4,3,2,1,0:T(8,128)} %collective-permute-done.1, f32[1,2,8,128,128]{4,3,2,1,0:T(8,128)S(1)} %copy-done.2, f32[1,1,8,128,128]{4,3,2,1,0:T(8,128)} %collective-permute-done), kind=kLoop, calls=%fused_computation.12 | loop fusion | flops 1048576 | bytes 4194304
  20.1 2.2 %fusion.5 = f32[16,128,128]{2,0,1:T(8,128)S(1)} fusion(f32[16,32]{1,0:T(8,128)S(1)} %select_reduce_fusion, f32[4,8,128,128]{3,2,1,0:T(8,128)S(1)} %maximum_bitcast_fusion), kind=kOutput, calls=%fused_computation.9 | convolution fusion | flops 100663296 | bytes 3147776 | tf_op jit(solution)/shard_map/while/body/eval_jaxpr/dot_general | solution.py:127
  22.4 0.3 pad_maximum_fusion.1
  22.7 0.5 copy-done.4
  23.2 5.3 %convolution_bitcast_fusion.2 = f32[32,2,128,128]{3,2,0,1:T(8,128)S(1)} fusion(f32[32,128,128]{2,0,1:T(8,128)S(1)} %pad_maximum_fusion.1, f32[128,1,128]{2,0,1:T(8,128)} %scatter.10, f32[128,1,128]{2,0,1:T(8,128)S(1)} %copy-done.4), kind=kOutput, calls=%fused_computation.6 | convolution fusion | flops 1610645504 | bytes 6422528 | tf_op jit(solution)/shard_map/while/body/eval_jaxpr/tab,bpl->tpal/dot_general | solution.py:75
  28.6 2.2 %copy.113 = f32[32,2,128,128]{3,2,1,0:T(8,128)} copy(f32[32,2,128,128]{3,2,0,1:T(8,128)S(1)} %convolution_bitcast_fusion.2) | data formatting | bytes 8388608 | tf_op jit(solution)/shard_map/while/body/eval_jaxpr/tab,bpl->tpal/transpose | solution.py:75
  30.8 5.5 %copy.128 = f32[32,256,128]{1,0,2:T(8,128)} copy(f32[32,256,128]{2,1,0:T(8,128)} %bitcast.121) | data formatting | bytes 8388608 | tf_op jit(solution)/shard_map/while/body/eval_jaxpr/reshape | solution.py:76
  36.3 9.8 %convolution_bitcast_fusion = f32[32,512,128]{1,0,2:T(8,128)S(1)} fusion(f32[32,256,128]{1,0,2:T(8,128)} %copy.128, f32[256,128]{1,0:T(8,128)S(1)} %get-tuple-element.109, f32[256,128]{1,0:T(8,128)S(1)} %fusion.68, f32[256,128]{1,0:T(8,128)S(1)} %get-tuple-element.108), kind=kOutput, calls=%fused_computation.3 | convolution fusion | flops 6442844160 | bytes 12976128 | tf_op jit(solution)/shard_map/while/body/eval_jaxpr/oq,tql->tol/dot_general | solution.py:77
  46.1 3.2 %copy-done.1 = f32[32,512,128]{1,0,2:T(8,128)} copy-done((f32[32,512,128]{1,0,2:T(8,128)}, f32[32,512,128]{1,0,2:T(8,128)S(1)}, u32[]{:S(2)}) %copy-start.1) | copy-done | bytes 8388632
  49.3 0.1 slice.271
  49.4 0.1 slice.268
  49.5 0.1 slice.265
  49.6 0.1 slice.262
  49.6 0.1 reverse.9
  49.8 0.1 slice_bitcast_fusion.10
  49.9 0.1 reverse.8
  50.0 0.1 slice_bitcast_fusion.11
  50.1 0.1 reverse.11
  50.2 0.1 slice_bitcast_fusion.8
  50.3 0.1 reverse.10
  50.5 0.1 slice_bitcast_fusion.9
  50.5 0.9 add_bitcast_fusion
  51.4 0.9 subtract_bitcast_fusion
  52.3 4.0 %subtract_select_fusion = (f32[16,256,128]{1,0,2:T(8,128)S(1)}, f32[16,256,128]{1,0,2:T(8,128)S(1)}) fusion(f32[32,512,128]{1,0,2:T(8,128)} %copy-done.1, f32[16,256]{1,0:T(8,128)S(1)} %subtract_bitcast_fusion, pred[128]{0:T(512)(128)(4,1)S(1)} %iota_compare_fusion.1, f32[16,256]{1,0:T(8,128)S(1)} %add_bitcast_fusion), kind=kLoop, calls=%fused_computation.17 | loop fusion | flops 4194304 | bytes 12615808 | tf_op jit(solution)/shard_map/while/body/eval_jaxpr/jit(_where)/select_n | solution.py:103
  56.3 0.6 pad_maximum_fusion
  56.9 6.4 %fusion.2 = f32[16,512,128]{1,2,0:T(8,128)} fusion(f32[16,512,128]{1,0,2:T(8,128)S(1)} %pad_maximum_fusion, f32[256,256]{1,0:T(8,128)S(1)} %get-tuple-element.111, f32[256,256]{1,0:T(8,128)S(1)} %get-tuple-element.110, f32[256,256]{1,0:T(8,128)S(1)} %fusion.58), kind=kOutput, calls=%fused_computation.7 | convolution fusion | flops 3222011904 | bytes 9175040 | tf_op jit(solution)/shard_map/while/body/eval_jaxpr/oq,tql->tol/dot_general | solution.py:111
  63.2 5.9 %reshape.394 = f32[16,2,256,128]{2,1,3,0:T(2,128)} reshape(f32[16,512,128]{1,2,0:T(8,128)} %fusion.2) | data formatting | bytes 8388608 | tf_op jit(solution)/shard_map/while/body/eval_jaxpr/reshape | solution.py:112
  69.1 7.3 %copy.121 = f32[16,256,128,2]{2,1,3,0:T(8,128)} copy(f32[16,256,128,2]{1,3,2,0:T(2,128)} %bitcast.122) | data formatting | bytes 8388608 | tf_op jit(solution)/shard_map/while/body/eval_jaxpr/tpml,pln->tmn/dot_general | solution.py:113
  76.4 4.1 %convolution_bitcast_fusion.1 = f32[2,8,256,256]{2,3,1,0:T(8,128)S(1)} fusion(f32[2,8,256,128,2]{3,2,4,1,0:T(8,128)} %bitcast.120, f32[1,128,256]{1,2,0:T(8,128)S(1)} %scatter.14, f32[1,128,256]{1,2,0:T(8,128)S(1)} %scatter.11), kind=kOutput, calls=%fused_computation.5 | convolution fusion | flops 1610743808 | bytes 8650752 | tf_op jit(solution)/shard_map/while/body/eval_jaxpr/tpml,pln->tmn/dot_general | solution.py:113
  80.5 0.4 fusion.79
  80.9 0.3 pad_add_fusion
  81.2 0.1 fusion.80
  81.4 0.3 copy.133
  81.7 0.3 copy.134
  82.0 0.2 pad_add_fusion.1
  82.3 1.9 %collective-permute-start.2 = (f32[1,64,1024]{2,1,0:T(8,128)S(1)}, f32[1,64,1024]{2,1,0:T(8,128)S(1)}, u32[]{:S(2)}, u32[]{:S(2)}) collective-permute-start(f32[1,64,1024]{2,1,0:T(8,128)S(1)} %get-tuple-element.103), channel_id=1, source_target_pairs={{0,1},{1,2},{2,3},{3,4},{4,5},{5,6},{6,7},{8,9},{9,10},{10,11},{11... | collective-permute-start | bytes 786440 | tf_op jit(solution)/shard_map/ppermute | solution.py:32
  84.2 3.6 %collective-permute-start.3 = (f32[1,64,1024]{2,1,0:T(8,128)S(1)}, f32[1,64,1024]{2,1,0:T(8,128)S(1)}, u32[]{:S(2)}, u32[]{:S(2)}) collective-permute-start(f32[1,64,1024]{2,1,0:T(8,128)S(1)} %get-tuple-element.102), channel_id=1, source_target_pairs={{1,0},{2,1},{3,2},{4,3},{5,4},{6,5},{7,6},{9,8},{10,9},{11,10},{12... | collective-permute-start | bytes 786440 | tf_op jit(solution)/shard_map/ppermute | solution.py:32
  87.9 2.0 %collective-permute-done.2 = f32[1,64,1024]{2,1,0:T(8,128)S(1)} collective-permute-done((f32[1,64,1024]{2,1,0:T(8,128)S(1)}, f32[1,64,1024]{2,1,0:T(8,128)S(1)}, u32[]{:S(2)}, u32[]{:S(2)}) %collective-permute-start.2) | collective-permute-done | bytes 262176 | tf_op jit(solution)/shard_map/ppermute | solution.py:32
  90.0 1.7 %collective-permute-done.3 = f32[1,64,1024]{2,1,0:T(8,128)S(1)} collective-permute-done((f32[1,64,1024]{2,1,0:T(8,128)S(1)}, f32[1,64,1024]{2,1,0:T(8,128)S(1)}, u32[]{:S(2)}, u32[]{:S(2)}) %collective-permute-start.3) | collective-permute-done | bytes 262176 | tf_op jit(solution)/shard_map/ppermute | solution.py:32
  91.8 40.0 %all_to_all.5 = f32[1,32,8,1024]{3,2,0,1:T(8,128)S(1)} all-to-all(f32[1,32,8,1024]{3,2,0,1:T(8,128)S(1)} %bitcast.127), channel_id=1, replica_groups=mesh['wave'=32,'tile'=8] {'wave'}, dimensions={1} | all-to-all | bytes 2097152 | tf_op jit(solution)/shard_map/all_to_all | solution.py:183
  131.8 1.2 convolution_bitcast_fusion.3
  133.0 0.7 copy.126
  (32 shorter events, 0.4 us)
Async XLA Ops:
  0.0 131.7 %copy-start = (f32[3,32]{1,0:T(4,128)S(1)}, f32[3,32]{1,0:T(4,128)}, u32[]{:S(2)}) copy-start(f32[3,32]{1,0:T(4,128)} %param.19) | copy-start | bytes 1156
  0.0 12.5 %copy-start.5 = (s32[2,8,4]{1,2,0:T(4,128)S(1)}, s32[2,8,4]{1,2,0:T(4,128)}, u32[]{:S(2)}) copy-start(s32[2,8,4]{1,2,0:T(4,128)} %param.17) | copy-start | bytes 772
  0.0 12.7 %copy-start.6 = (s32[2,8,4]{1,2,0:T(4,128)S(1)}, s32[2,8,4]{1,2,0:T(4,128)}, u32[]{:S(2)}) copy-start(s32[2,8,4]{1,2,0:T(4,128)} %param.18) | copy-start | bytes 772
  0.0 13.5 %copy-start.3 = (f32[1,256,1024]{2,1,0:T(8,128)S(1)}, f32[1,256,1024]{2,1,0:T(8,128)}, u32[]{:S(2)}) copy-start(f32[1,256,1024]{2,1,0:T(8,128)} %param.15) | copy-start | bytes 3145732
  2.4 16.2 %collective-permute-start = (f32[1,1,8,128,128]{4,3,2,1,0:T(8,128)}, f32[1,1,8,128,128]{4,3,2,1,0:T(8,128)}, u32[]{:S(2)}, u32[]{:S(2)}) collective-permute-start(f32[1,1,8,128,128]{4,3,2,1,0:T(8,128)} %get-tuple-element.104), channel_id=1, source_target_pairs={{0,1},{1,2},{2,3},{3,4},{4,5},{5,6},{6,7},{8,9},{9,10},{10,11},{11... | collective-permute-start | bytes 1572872 | tf_op jit(solution)/shard_map/ppermute | solution.py:20
  4.3 14.3 %collective-permute-start.1 = (f32[1,1,8,128,128]{4,3,2,1,0:T(8,128)}, f32[1,1,8,128,128]{4,3,2,1,0:T(8,128)}, u32[]{:S(2)}, u32[]{:S(2)}) collective-permute-start(f32[1,1,8,128,128]{4,3,2,1,0:T(8,128)} %get-tuple-element.105), channel_id=1, source_target_pairs={{1,0},{2,1},{3,2},{4,3},{5,4},{6,5},{7,6},{9,8},{10,9},{11,10},{12... | collective-permute-start | bytes 1572872 | tf_op jit(solution)/shard_map/ppermute | solution.py:22
  13.7 5.0 %copy-start.2 = (f32[1,2,8,128,128]{4,3,2,1,0:T(8,128)S(1)}, f32[1,2,8,128,128]{4,3,2,1,0:T(8,128)}, u32[]{:S(2)}) copy-start(f32[1,2,8,128,128]{4,3,2,1,0:T(8,128)} %param.16) | copy-start | bytes 3145732
  22.4 0.8 copy-start.4
  46.1 3.2 %copy-start.1 = (f32[32,512,128]{1,0,2:T(8,128)}, f32[32,512,128]{1,0,2:T(8,128)S(1)}, u32[]{:S(2)}) copy-start(f32[32,512,128]{1,0,2:T(8,128)S(1)} %convolution_bitcast_fusion) | copy-start | bytes 25165828
  82.3 7.7 %collective-permute-start.2 = (f32[1,64,1024]{2,1,0:T(8,128)S(1)}, f32[1,64,1024]{2,1,0:T(8,128)S(1)}, u32[]{:S(2)}, u32[]{:S(2)}) collective-permute-start(f32[1,64,1024]{2,1,0:T(8,128)S(1)} %get-tuple-element.103), channel_id=1, source_target_pairs={{0,1},{1,2},{2,3},{3,4},{4,5},{5,6},{6,7},{8,9},{9,10},{10,11},{11... | collective-permute-start | bytes 786440 | tf_op jit(solution)/shard_map/ppermute | solution.py:32
  84.2 7.5 %collective-permute-start.3 = (f32[1,64,1024]{2,1,0:T(8,128)S(1)}, f32[1,64,1024]{2,1,0:T(8,128)S(1)}, u32[]{:S(2)}, u32[]{:S(2)}) collective-permute-start(f32[1,64,1024]{2,1,0:T(8,128)S(1)} %get-tuple-element.102), channel_id=1, source_target_pairs={{1,0},{2,1},{3,2},{4,3},{5,4},{6,5},{7,6},{9,8},{10,9},{11,10},{12... | collective-permute-start | bytes 786440 | tf_op jit(solution)/shard_map/ppermute | solution.py:32

commit v3 on v2

--- a/solution.py
+++ b/solution.py
@@ -69,13 +69,14 @@
 
 
 def forward(blocks, first, rows_fwd):
-    tiles, side = blocks.shape[0], blocks.shape[1]
+    tiles = blocks.shape[0]
     half = first.shape[-1]
     length = rows_fwd.shape[0] // 2
-    packed = jnp.einsum("tab,bpl->tpal", blocks, first, precision=highest)
-    packed = packed.reshape(tiles, 2 * side, half)
-    spec = jnp.einsum("oq,tql->tol", rows_fwd, packed, precision=highest)
-    return spec[:, :length], spec[:, length:]
+    first = first.transpose(0, 2, 1).reshape(first.shape[0], 2 * half)
+    packed = jnp.einsum("tab,bj->tja", blocks, first, precision=highest)
+    packed = packed.reshape(tiles, half, rows_fwd.shape[1])
+    spec = jnp.einsum("tlq,oq->tlo", packed, rows_fwd, precision=highest)
+    return spec[..., :length], spec[..., length:]
 
 
 def reverse(values):
@@ -95,22 +96,23 @@
 
 def product(scene_spec, psf_spec):
     prod_real, prod_imag = times(scene_spec, psf_spec)
-    scene_low, scene_top = split_packed(scene_spec[0][..., 0], scene_spec[1][..., 0])
-    psf_low, psf_top = split_packed(psf_spec[0][..., 0], psf_spec[1][..., 0])
+    scene_low, scene_top = split_packed(scene_spec[0][:, 0], scene_spec[1][:, 0])
+    psf_low, psf_top = split_packed(psf_spec[0][:, 0], psf_spec[1][:, 0])
     low = times(scene_low, psf_low)
     top = times(scene_top, psf_top)
-    first_column = lax.iota(jnp.int32, prod_real.shape[-1]) == 0
-    prod_real = jnp.where(first_column, (low[0] - top[1])[..., None], prod_real)
-    prod_imag = jnp.where(first_column, (low[1] + top[0])[..., None], prod_imag)
+    first_column = (lax.iota(jnp.int32, prod_real.shape[1]) == 0)[:, None]
+    prod_real = jnp.where(first_column, (low[0] - top[1])[:, None, :], prod_real)
+    prod_imag = jnp.where(first_column, (low[1] + top[0])[:, None, :], prod_imag)
     return prod_real, prod_imag
 
 
 def inverse(prod_real, prod_imag, rows_inv, last):
-    tiles, length, half = prod_real.shape
-    stacked = jnp.concatenate([prod_real, prod_imag], axis=1)
-    both = jnp.einsum("oq,tql->tol", rows_inv, stacked, precision=high)
-    both = both.reshape(tiles, 2, length, half)
-    return jnp.einsum("tpml,pln->tmn", both, last, precision=high)
+    tiles, half, length = prod_real.shape
+    stacked = jnp.concatenate([prod_real, prod_imag], axis=-1)
+    rows_inv = rows_inv.reshape(2, length, 2 * length).transpose(1, 0, 2).reshape(2 * length, 2 * length)
+    both = jnp.einsum("tlq,oq->tol", stacked, rows_inv, precision=high)
+    both = both.reshape(tiles, length, 2 * half)
+    return jnp.einsum("tmj,jn->tmn", both, last.reshape(2 * half, length), precision=high)
 
 
 def blur_wave(scene_plane, extended_plane, mixing, tables):

time: 135 us -> 127 us (0.941)
  local copies, waits for them, and re-layouts: 33.5 us -> 25.1 us
    reshape x2, local copies, waits for them, and re-layouts: 11.4 us -> 5.97 us  [the longest x1 5.25 us: forward(): packed = packed.reshape(tiles, half, rows_fwd.shape[1])]
    dot_general x1, local copies, waits for them, and re-layouts: 7.26 us -> 5.24 us  [inverse(): jnp.einsum('tmj,jn->tmn', both, last.reshape(2 * half, length), precision...]
    broadcast_in_dim x2, other arithmetic: 1.74 us -> 0.21 us  [the longest x1 0.12 us: product(): jnp.where(first_column, (low[1] + top[0])[:, None, :], prod_imag)]
    unnamed x21 -> x33, local copies, waits for them, and re-layouts: 5.2 us -> 5.95 us
  transfers between devices with their start and end apart: 4 -> 4, of which waited for: 2 -> 2; matrix products, arithmetic and copies ran while one was open for 8% -> 11% of each run, Pallas kernels for 0% -> 0%
where the time goes in v3:
time: 127 us; the launch traced here: 125 us
  blocking collectives  40 us (31%)
  matrix products  28.7 us (23%)
  local copies, waits for them, and re-layouts  25.1 us (20%)
  other arithmetic  16.2 us (13%)
  starting transfers between devices  11.2 us (9%)
  waiting for transfers between devices  3.75 us (3%)
    all_to_all x1, blocking collectives, per_device(): gathered = lax.all_to_all(pieces, 'wave', 1, 1, tiled=True)  40 us
    dot_general x1, matrix products, forward(): spec = jnp.einsum('tlq,oq->tlo', packed, rows_fwd, precision=highest)  9.12 us
    dot_general x1, matrix products, forward(): packed = jnp.einsum('tab,bj->tja', blocks, first, precision=highest)  6.82 us
    unnamed x33, local copies, waits for them, and re-layouts  5.95 us
    ppermute x2, starting transfers between devices, from_behind(): return lax.ppermute(shard, axis, pairs)  5.56 us
    reshape x1, local copies, waits for them, and re-layouts, forward(): packed = packed.reshape(tiles, half, rows_fwd.shape[1])  5.25 us
    dot_general x1, local copies, waits for them, and re-layouts, inverse(): jnp.einsum('tmj,jn->tmn', both, last.reshape(2 * half, length), precision...  5.24 us
    dot_general x1, matrix products, inverse(): both = jnp.einsum('tlq,oq->tol', stacked, rows_inv, precision=high)  5.13 us
  transfers between devices with their start and end apart: 4, of which 2 were waited for; matrix products, arithmetic and copies ran while one was open for 11% of the time, Pallas kernels for 0%

profile of v3, /device:TPU:8, one launch (start us, length us, event | category | flops | bytes accessed | tf_op | source)
XLA Modules:
  0.0 125.4 jit_solution(9170060642342516799)
XLA Ops:
  0.0 2.3 %fusion.64 = (f32[1,1,8,128,128]{4,3,2,1,0:T(8,128)}, f32[1,1,8,128,128]{4,3,2,1,0:T(8,128)}) fusion(f32[1,2,8,128,128]{4,3,2,1,0:T(8,128)} %param.16), kind=kLoop, calls=%fused_computation.131 | loop fusion | bytes 2097152 | tf_op jit(solution)/shard_map/slice | solution.py:17
  2.3 2.0 %collective-permute-start = (f32[1,1,8,128,128]{4,3,2,1,0:T(8,128)}, f32[1,1,8,128,128]{4,3,2,1,0:T(8,128)}, u32[]{:S(2)}, u32[]{:S(2)}) collective-permute-start(f32[1,1,8,128,128]{4,3,2,1,0:T(8,128)} %get-tuple-element.104), channel_id=1, source_target_pairs={{0,1},{1,2},{2,3},{3,4},{4,5},{5,6},{6,7},{8,9},{9,10},{10,11},{11... | collective-permute-start | bytes 1572872 | tf_op jit(solution)/shard_map/ppermute | solution.py:20
  4.4 3.6 %collective-permute-start.1 = (f32[1,1,8,128,128]{4,3,2,1,0:T(8,128)}, f32[1,1,8,128,128]{4,3,2,1,0:T(8,128)}, u32[]{:S(2)}, u32[]{:S(2)}) collective-permute-start(f32[1,1,8,128,128]{4,3,2,1,0:T(8,128)} %get-tuple-element.105), channel_id=1, source_target_pairs={{1,0},{2,1},{3,2},{4,3},{5,4},{6,5},{7,6},{9,8},{10,9},{11,10},{12... | collective-permute-start | bytes 1572872 | tf_op jit(solution)/shard_map/ppermute | solution.py:22
  8.1 0.6 compare_reduce_fusion
  8.8 0.3 sine_negate_fusion
  9.0 0.3 fusion.53
  9.3 0.5 fusion.52
  9.8 1.0 fusion.38
  10.8 1.0 fusion.42
  11.8 1.2 cosine_multiply_fusion
  13.0 0.5 sine_multiply_fusion
  13.5 0.1 sub.62
  13.6 0.1 div.18
  13.7 0.7 fusion.57
  14.4 0.1 copy.120
  14.5 0.1 select_reduce_fusion
  14.6 0.3 scatter.10
  14.9 0.1 maximum_maximum_fusion
  15.0 0.5 iota_compare_fusion.1
  15.5 0.2 copy.150
  15.7 0.8 copy.121
  16.5 0.8 copy.119
  17.3 0.7 reshape.424
  18.0 1.4 %scatter.11 = f32[1,128,256]{2,1,0:T(8,128)} dynamic-update-slice(f32[1,128,256]{2,1,0:T(8,128)} %cosine_multiply_fusion, f32[1,1,256]{2,1,0:T(1,128)S(1)} %stack.16, s32[]{:T(128)} %constant.227.clone.1, s32[]{:T(128)} %constant.227.clone.1, s32[]{:T(128)} %constant.227.clone.1) | dynamic-update-slice | bytes 2052 | tf_op jit(solution)/shard_map/scatter | solution.py:65
  19.5 0.6 copy-done.7
  20.1 1.2 fusion.47
  21.4 1.0 maximum_multiply_fusion
  22.4 0.1 copy_bitcast_fusion
  22.5 1.5 %maximum_bitcast_fusion = f32[4,8,128,128]{3,2,1,0:T(8,128)S(1)} fusion(f32[1,1,8,128,128]{4,3,2,1,0:T(8,128)} %collective-permute-done.1, f32[1,2,8,128,128]{4,3,2,1,0:T(8,128)S(1)} %copy-done.2, f32[1,1,8,128,128]{4,3,2,1,0:T(8,128)} %collective-permute-done), kind=kLoop, calls=%fused_computation.11 | loop fusion | flops 1048576 | bytes 4194304
  23.9 2.2 %fusion.7 = f32[16,128,128]{2,0,1:T(8,128)S(1)} fusion(f32[16,32]{1,0:T(8,128)S(1)} %select_reduce_fusion, f32[4,8,128,128]{3,2,1,0:T(8,128)S(1)} %maximum_bitcast_fusion), kind=kOutput, calls=%fused_computation.8 | convolution fusion | flops 100663296 | bytes 3147776 | tf_op jit(solution)/shard_map/while/body/eval_jaxpr/dot_general | solution.py:129
  26.2 0.3 pad_maximum_fusion
  26.5 0.6 copy-done.6
  27.1 6.8 %convolution_bitcast_fusion = f32[32,256,128]{2,1,0:T(8,128)} fusion(f32[128,256,1]{0,1,2:T(8,128)S(1)} %bitcast.121, f32[32,128,128]{2,0,1:T(8,128)S(1)} %pad_maximum_fusion), kind=kOutput, calls=%fused_computation.6 | convolution fusion | flops 1610612736 | bytes 6422528 | tf_op jit(solution)/shard_map/while/body/eval_jaxpr/tab,bj->tja/dot_general | solution.py:76
  33.9 5.3 %reshape.417 = f32[32,128,256]{2,1,0:T(8,128)} reshape(f32[32,256,128]{2,1,0:T(8,128)} %convolution_bitcast_fusion) | data formatting | bytes 8388608 | tf_op jit(solution)/shard_map/while/body/eval_jaxpr/reshape | solution.py:77
  39.2 9.1 %fusion.13 = f32[32,128,512]{2,1,0:T(8,128)S(1)} fusion(f32[32,128,256]{2,1,0:T(8,128)} %reshape.417, f32[256,128]{1,0:T(8,128)S(1)} %copy-done.5, f32[256,128]{1,0:T(8,128)S(1)} %fusion.52, f32[256,128]{1,0:T(8,128)S(1)} %copy-done.4), kind=kOutput, calls=%fused_computation.23 | convolution fusion | flops 6442844160 | bytes 12976128 | tf_op jit(solution)/shard_map/while/body/eval_jaxpr/tlq,oq->tlo/dot_general | solution.py:78
  48.3 3.2 %copy-done.1 = f32[32,128,512]{2,1,0:T(8,128)} copy-done((f32[32,128,512]{2,1,0:T(8,128)}, f32[32,128,512]{2,1,0:T(8,128)S(1)}, u32[]{:S(2)}) %copy-start.1) | copy-done | bytes 8388632
  51.7 0.1 slice.268
  51.8 0.1 slice.265
  51.8 0.1 slice.262
  51.9 0.1 reverse.11
  52.1 0.1 slice_bitcast_fusion.4
  52.1 0.1 reverse.10
  52.4 0.1 reverse.9
  52.6 0.1 reverse.8
  52.7 0.1 slice_bitcast_fusion.7
  52.8 0.1 add_bitcast_fusion
  52.9 0.1 subtract_bitcast_fusion
  53.0 4.6 %subtract_select_fusion = (f32[16,128,256]{2,1,0:T(8,128)S(1)}, f32[16,128,256]{2,1,0:T(8,128)S(1)}) fusion(f32[32,128,512]{2,1,0:T(8,128)} %copy-done.1, f32[16,256]{1,0:T(8,128)S(1)} %subtract_bitcast_fusion, pred[128]{0:T(512)(128)(4,1)S(1)} %copy-done.10, f32[16,256]{1,0:T(8,128)S(1)} %add_bitcast_fusion), kind=kLoop, calls=%fused_computation.15 | loop fusion | flops 4194304 | bytes 12615808 | tf_op jit(solution)/shard_map/while/body/eval_jaxpr/jit(_where)/select_n | solution.py:104
  57.6 5.1 %fusion.4 = f32[16,512,128]{2,1,0:T(8,128)} fusion(f32[512,512,1]{1,0,2:T(8,128)S(1)} %reshape.424, f32[16,128,256]{2,1,0:T(8,128)S(1)} %get-tuple-element.93, f32[16,128,256]{2,1,0:T(8,128)S(1)} %get-tuple-element.92), kind=kOutput, calls=%fused_computation.5 | convolution fusion | flops 3222274048 | bytes 9437184 | tf_op jit(solution)/shard_map/while/body/eval_jaxpr/tlq,oq->tol/dot_general | solution.py:113
  62.7 5.2 %dot_general.37 = f32[2,8,256,256]{3,2,1,0:T(8,128)} reshape(f32[16,512,128]{2,1,0:T(8,128)} %fusion.4) | data formatting | bytes 8388608 | tf_op jit(solution)/shard_map/while/body/eval_jaxpr/tmj,jn->tmn/dot_general | solution.py:115
  68.0 4.2 %fusion.65 = f32[2,8,256,256]{2,3,1,0:T(8,128)S(1)} fusion(f32[2,8,256,256]{3,2,1,0:T(8,128)} %dot_general.37, f32[256,256,1,1]{1,0,3,2:T(8,128)S(1)} %bitcast.119), kind=kOutput, calls=%fused_computation.136 | convolution fusion | flops 1610612736 | bytes 8650752 | tf_op jit(solution)/shard_map/while/body/eval_jaxpr/tmj,jn->tmn/dot_general | solution.py:115
  72.2 0.4 fusion.61
  72.6 0.3 pad_add_fusion
  72.9 0.1 fusion.62
  73.0 0.3 copy.147
  73.4 0.3 copy.148
  73.7 0.2 pad_add_fusion.1
  74.0 1.9 %collective-permute-start.2 = (f32[1,64,1024]{2,1,0:T(8,128)S(1)}, f32[1,64,1024]{2,1,0:T(8,128)S(1)}, u32[]{:S(2)}, u32[]{:S(2)}) collective-permute-start(f32[1,64,1024]{2,1,0:T(8,128)S(1)} %get-tuple-element.103), channel_id=1, source_target_pairs={{0,1},{1,2},{2,3},{3,4},{4,5},{5,6},{6,7},{8,9},{9,10},{10,11},{11... | collective-permute-start | bytes 786440 | tf_op jit(solution)/shard_map/ppermute | solution.py:32
  75.9 3.6 %collective-permute-start.3 = (f32[1,64,1024]{2,1,0:T(8,128)S(1)}, f32[1,64,1024]{2,1,0:T(8,128)S(1)}, u32[]{:S(2)}, u32[]{:S(2)}) collective-permute-start(f32[1,64,1024]{2,1,0:T(8,128)S(1)} %get-tuple-element.102), channel_id=1, source_target_pairs={{1,0},{2,1},{3,2},{4,3},{5,4},{6,5},{7,6},{9,8},{10,9},{11,10},{12... | collective-permute-start | bytes 786440 | tf_op jit(solution)/shard_map/ppermute | solution.py:32
  79.6 2.0 %collective-permute-done.2 = f32[1,64,1024]{2,1,0:T(8,128)S(1)} collective-permute-done((f32[1,64,1024]{2,1,0:T(8,128)S(1)}, f32[1,64,1024]{2,1,0:T(8,128)S(1)}, u32[]{:S(2)}, u32[]{:S(2)}) %collective-permute-start.2) | collective-permute-done | bytes 262176 | tf_op jit(solution)/shard_map/ppermute | solution.py:32
  81.7 1.7 %collective-permute-done.3 = f32[1,64,1024]{2,1,0:T(8,128)S(1)} collective-permute-done((f32[1,64,1024]{2,1,0:T(8,128)S(1)}, f32[1,64,1024]{2,1,0:T(8,128)S(1)}, u32[]{:S(2)}, u32[]{:S(2)}) %collective-permute-start.3) | collective-permute-done | bytes 262176 | tf_op jit(solution)/shard_map/ppermute | solution.py:32
  83.5 40.0 %all_to_all.5 = f32[1,32,8,1024]{3,2,0,1:T(8,128)S(1)} all-to-all(f32[1,32,8,1024]{3,2,0,1:T(8,128)S(1)} %bitcast.116), channel_id=1, replica_groups=mesh['wave'=32,'tile'=8] {'wave'}, dimensions={1} | all-to-all | bytes 2097152 | tf_op jit(solution)/shard_map/all_to_all | solution.py:185
  123.5 1.2 convolution_bitcast_fusion.1
  124.7 0.7 copy.140
  (47 shorter events, 0.7 us)
Async XLA Ops:
  0.0 123.5 %copy-start = (f32[3,32]{1,0:T(4,128)S(1)}, f32[3,32]{1,0:T(4,128)}, u32[]{:S(2)}) copy-start(f32[3,32]{1,0:T(4,128)} %param.19) | copy-start | bytes 1156
  0.0 13.5 %copy-start.8 = (s32[2,8,4]{1,2,0:T(4,128)S(1)}, s32[2,8,4]{1,2,0:T(4,128)}, u32[]{:S(2)}) copy-start(s32[2,8,4]{1,2,0:T(4,128)} %param.17) | copy-start | bytes 772
  0.0 13.6 %copy-start.9 = (s32[2,8,4]{1,2,0:T(4,128)S(1)}, s32[2,8,4]{1,2,0:T(4,128)}, u32[]{:S(2)}) copy-start(s32[2,8,4]{1,2,0:T(4,128)} %param.18) | copy-start | bytes 772
  2.3 13.2 %copy-start.3 = (f32[1,256,1024]{2,1,0:T(8,128)S(1)}, f32[1,256,1024]{2,1,0:T(8,128)}, u32[]{:S(2)}) copy-start(f32[1,256,1024]{2,1,0:T(8,128)} %param.15) | copy-start | bytes 3145732
  2.3 20.1 %collective-permute-start = (f32[1,1,8,128,128]{4,3,2,1,0:T(8,128)}, f32[1,1,8,128,128]{4,3,2,1,0:T(8,128)}, u32[]{:S(2)}, u32[]{:S(2)}) collective-permute-start(f32[1,1,8,128,128]{4,3,2,1,0:T(8,128)} %get-tuple-element.104), channel_id=1, source_target_pairs={{0,1},{1,2},{2,3},{3,4},{4,5},{5,6},{6,7},{8,9},{9,10},{10,11},{11... | collective-permute-start | bytes 1572872 | tf_op jit(solution)/shard_map/ppermute | solution.py:20
  4.4 18.1 %collective-permute-start.1 = (f32[1,1,8,128,128]{4,3,2,1,0:T(8,128)}, f32[1,1,8,128,128]{4,3,2,1,0:T(8,128)}, u32[]{:S(2)}, u32[]{:S(2)}) collective-permute-start(f32[1,1,8,128,128]{4,3,2,1,0:T(8,128)} %get-tuple-element.105), channel_id=1, source_target_pairs={{1,0},{2,1},{3,2},{4,3},{5,4},{6,5},{7,6},{9,8},{10,9},{11,10},{12... | collective-permute-start | bytes 1572872 | tf_op jit(solution)/shard_map/ppermute | solution.py:22
  18.0 4.4 %copy-start.2 = (f32[1,2,8,128,128]{4,3,2,1,0:T(8,128)S(1)}, f32[1,2,8,128,128]{4,3,2,1,0:T(8,128)}, u32[]{:S(2)}) copy-start(f32[1,2,8,128,128]{4,3,2,1,0:T(8,128)} %param.16) | copy-start | bytes 3145732
  19.5 0.7 copy-start.7
  26.2 0.9 copy-start.6
  33.9 5.3 %copy-start.4 = (f32[256,128]{1,0:T(8,128)S(1)}, f32[256,128]{1,0:T(8,128)}, u32[]{:S(2)}) copy-start(f32[256,128]{1,0:T(8,128)} %get-tuple-element.110) | copy-start | bytes 393220
  33.9 5.3 %copy-start.5 = (f32[256,128]{1,0:T(8,128)S(1)}, f32[256,128]{1,0:T(8,128)}, u32[]{:S(2)}) copy-start(f32[256,128]{1,0:T(8,128)} %get-tuple-element.111) | copy-start | bytes 393220
  39.2 13.9 %copy-start.10 = (pred[128]{0:T(512)(128)(4,1)S(1)}, pred[128]{0:T(512)(128)(4,1)}, u32[]{:S(2)}) copy-start(pred[128]{0:T(512)(128)(4,1)} %iota_compare_fusion.1) | copy-start | bytes 388
  48.3 3.2 %copy-start.1 = (f32[32,128,512]{2,1,0:T(8,128)}, f32[32,128,512]{2,1,0:T(8,128)S(1)}, u32[]{:S(2)}) copy-start(f32[32,128,512]{2,1,0:T(8,128)S(1)} %fusion.13) | copy-start | bytes 25165828
  74.0 7.7 %collective-permute-start.2 = (f32[1,64,1024]{2,1,0:T(8,128)S(1)}, f32[1,64,1024]{2,1,0:T(8,128)S(1)}, u32[]{:S(2)}, u32[]{:S(2)}) collective-permute-start(f32[1,64,1024]{2,1,0:T(8,128)S(1)} %get-tuple-element.103), channel_id=1, source_target_pairs={{0,1},{1,2},{2,3},{3,4},{4,5},{5,6},{6,7},{8,9},{9,10},{10,11},{11... | collective-permute-start | bytes 786440 | tf_op jit(solution)/shard_map/ppermute | solution.py:32
  75.9 7.5 %collective-permute-start.3 = (f32[1,64,1024]{2,1,0:T(8,128)S(1)}, f32[1,64,1024]{2,1,0:T(8,128)S(1)}, u32[]{:S(2)}, u32[]{:S(2)}) collective-permute-start(f32[1,64,1024]{2,1,0:T(8,128)S(1)} %get-tuple-element.102), channel_id=1, source_target_pairs={{1,0},{2,1},{3,2},{4,3},{5,4},{6,5},{7,6},{9,8},{10,9},{11,10},{12... | collective-permute-start | bytes 786440 | tf_op jit(solution)/shard_map/ppermute | solution.py:32

commit v4 on v3

--- a/solution.py
+++ b/solution.py
@@ -40,19 +40,15 @@
 
 def dft_tables(side):
     length = 2 * side
-    half = side
-    cos_in, sin_in = angle_table(side, half, length)
-    alternating = jnp.where(lax.iota(jnp.int32, side) % 2 == 0, 1.0, -1.0).astype(jnp.float32)
-    first = jnp.stack([cos_in, (-sin_in).at[:, 0].set(alternating)], axis=1)
-    cos_top, sin_top = angle_table(side, length, length)
-    rows_fwd = jnp.concatenate(
-        [
-            jnp.concatenate([cos_top.T, sin_top.T], axis=1),
-            jnp.concatenate([-sin_top.T, cos_top.T], axis=1),
-        ],
-        axis=0,
-    )
     cos_full, sin_full = angle_table(length, length, length)
+    first_row = (lax.iota(jnp.int32, side) == 0)
+    signs = jnp.where(lax.iota(jnp.int32, length) % 2 == 0, 1.0, -1.0).astype(jnp.float32)
+    cos_in, sin_in = cos_full[:side, :side], sin_full[:side, :side]
+    first = jnp.stack([cos_in, jnp.where(first_row[None, :], signs[:side, None], -sin_in)], axis=1)
+    cos_k, sin_k = cos_full[:, :side], sin_full[:, :side]
+    rows_fwd = jnp.stack(
+        [jnp.stack([cos_k, sin_k], axis=1), jnp.stack([-sin_k, cos_k], axis=1)], axis=0
+    ).reshape(2 * length, 2, side)
     rows_inv = jnp.concatenate(
         [
             jnp.concatenate([cos_full, -sin_full], axis=1),
@@ -60,22 +56,18 @@
         ],
         axis=0,
     )
-    cos_out, sin_out = angle_table(half, length, length)
-    every = jnp.where(lax.iota(jnp.int32, length) % 2 == 0, 1.0, -1.0).astype(jnp.float32)
-    cos_out = (2.0 * cos_out).at[0].set(1.0)
-    sin_out = (-2.0 * sin_out).at[0].set(every)
+    cos_out = jnp.where(first_row[:, None], 1.0, 2.0 * cos_full[:side])
+    sin_out = jnp.where(first_row[:, None], signs[None, :], -2.0 * sin_full[:side])
     last = jnp.stack([cos_out, sin_out], axis=0) / float(length * length)
     return first, rows_fwd, rows_inv, last
 
 
 def forward(blocks, first, rows_fwd):
-    tiles = blocks.shape[0]
-    half = first.shape[-1]
+    side = blocks.shape[1]
     length = rows_fwd.shape[0] // 2
-    first = first.transpose(0, 2, 1).reshape(first.shape[0], 2 * half)
-    packed = jnp.einsum("tab,bj->tja", blocks, first, precision=highest)
-    packed = packed.reshape(tiles, half, rows_fwd.shape[1])
-    spec = jnp.einsum("tlq,oq->tlo", packed, rows_fwd, precision=highest)
+    packed = jnp.einsum("tab,bpl->tpla", blocks, first, precision=highest)
+    rows_fwd = rows_fwd.reshape(2 * length, 2, side)
+    spec = jnp.einsum("tpla,opa->tlo", packed, rows_fwd, precision=highest)
     return spec[..., :length], spec[..., length:]
 
 
@@ -109,10 +101,9 @@
 def inverse(prod_real, prod_imag, rows_inv, last):
     tiles, half, length = prod_real.shape
     stacked = jnp.concatenate([prod_real, prod_imag], axis=-1)
-    rows_inv = rows_inv.reshape(2, length, 2 * length).transpose(1, 0, 2).reshape(2 * length, 2 * length)
     both = jnp.einsum("tlq,oq->tol", stacked, rows_inv, precision=high)
-    both = both.reshape(tiles, length, 2 * half)
-    return jnp.einsum("tmj,jn->tmn", both, last.reshape(2 * half, length), precision=high)
+    both = both.reshape(tiles, 2, length, half)
+    return jnp.einsum("tpml,pln->tmn", both, last, precision=high)
 
 
 def blur_wave(scene_plane, extended_plane, mixing, tables):

time: 127 us -> 104 us (0.82)
  local copies, waits for them, and re-layouts: 25.1 us -> 10.1 us
  other arithmetic: 16.2 us -> 10.4 us
  matrix products: 28.7 us -> 24.7 us
  waiting for transfers between devices: 3.75 us -> 5.42 us
    reshape x2 -> x0, local copies, waits for them, and re-layouts: 5.97 us -> none  [the longest x1 5.25 us: forward(): packed = packed.reshape(tiles, half, rows_fwd.shape[1])]
    dot_general x3, matrix products: 20.1 us -> 14.2 us  [the longest x1 7.62 us: forward(): spec = jnp.einsum('tpla,opa->tlo', packed, rows_fwd, precision=highest)]
    dot_general x1 -> x0, local copies, waits for them, and re-layouts: 5.24 us -> none  [inverse(): jnp.einsum('tmj,jn->tmn', both, last.reshape(2 * half, length), precision...]
    dot_general x1, matrix products: 5.13 us -> 7.05 us  [inverse(): both = jnp.einsum('tlq,oq->tol', stacked, rows_inv, precision=high)]
    scatter x3 -> x0, local copies, waits for them, and re-layouts: 1.69 us -> none  [the longest x1 1.4 us: dft_tables(): cos_out = (2.0 * cos_out).at[0].set(1.0)]
    mul x2 -> x0, other arithmetic: 1.65 us -> none  [the longest x1 1.15 us: dft_tables(): cos_out = (2.0 * cos_out).at[0].set(1.0)]
    ppermute x1, waiting for transfers between devices: 0.01 us -> 1.44 us  [with_halo(): lax.ppermute(head, axis, [((i + 1) % count, i) for i in range(ends)])]
    sin x2 -> x1, other arithmetic: 2.28 us -> 0.97 us  [angle_table(): return (jnp.cos(angles), jnp.sin(angles))]
  transfers between devices with their start and end apart: 4 -> 4, of which waited for: 2 -> 4; matrix products, arithmetic and copies ran while one was open for 11% -> 5% of each run, Pallas kernels for 0% -> 0%
where the time goes in v4:
time: 104 us; the launch traced here: 102 us
  blocking collectives  40 us (38%)
  matrix products  24.7 us (24%)
  starting transfers between devices  11.4 us (11%)
  other arithmetic  10.4 us (10%)
  local copies, waits for them, and re-layouts  10.1 us (10%)
  waiting for transfers between devices  5.42 us (5%)
    all_to_all x1, blocking collectives, per_device(): gathered = lax.all_to_all(pieces, 'wave', 1, 1, tiled=True)  40 us
    dot_general x1, matrix products, forward(): spec = jnp.einsum('tpla,opa->tlo', packed, rows_fwd, precision=highest)  7.62 us
    dot_general x1, matrix products, inverse(): both = jnp.einsum('tlq,oq->tol', stacked, rows_inv, precision=high)  7.05 us
    ppermute x2, starting transfers between devices, from_behind(): return lax.ppermute(shard, axis, pairs)  5.84 us
    unnamed x27, local copies, waits for them, and re-layouts  4.73 us
    dot_general x1, matrix products, forward(): packed = jnp.einsum('tab,bpl->tpla', blocks, first, precision=highest)  4.6 us
    select_n x1, other arithmetic, product(): jnp.where(first_column, (low[0] - top[1])[:, None, :], prod_real)  4.56 us
    ppermute x2, waiting for transfers between devices, from_behind(): return lax.ppermute(shard, axis, pairs)  3.75 us
  transfers between devices with their start and end apart: 4, of which 4 were waited for; matrix products, arithmetic and copies ran while one was open for 5% of the time, Pallas kernels for 0%

profile of v4, /device:TPU:8, one launch (start us, length us, event | category | flops | bytes accessed | tf_op | source)
XLA Modules:
  0.0 102.5 jit_solution(1094395801399016921)
XLA Ops:
  0.0 0.0 copy-start
  0.0 2.1 %fusion.56 = (f32[1,1,8,128,128]{4,3,2,1,0:T(8,128)}, f32[1,1,8,128,128]{4,3,2,1,0:T(8,128)S(1)}) fusion(f32[1,2,8,128,128]{4,3,2,1,0:T(8,128)} %param.10), kind=kLoop, calls=%fused_computation.110 | loop fusion | bytes 2097152 | tf_op jit(solution)/shard_map/slice | solution.py:17
  2.1 1.9 %collective-permute-start = (f32[1,1,8,128,128]{4,3,2,1,0:T(8,128)}, f32[1,1,8,128,128]{4,3,2,1,0:T(8,128)}, u32[]{:S(2)}, u32[]{:S(2)}) collective-permute-start(f32[1,1,8,128,128]{4,3,2,1,0:T(8,128)} %get-tuple-element.68), channel_id=1, source_target_pairs={{0,1},{1,2},{2,3},{3,4},{4,5},{5,6},{6,7},{8,9},{9,10},{10,11},{11... | collective-permute-start | bytes 1572872 | tf_op jit(solution)/shard_map/ppermute | solution.py:20
  4.0 3.6 %collective-permute-start.1 = (f32[1,1,8,128,128]{4,3,2,1,0:T(8,128)S(1)}, f32[1,1,8,128,128]{4,3,2,1,0:T(8,128)}, u32[]{:S(2)}, u32[]{:S(2)}) collective-permute-start(f32[1,1,8,128,128]{4,3,2,1,0:T(8,128)S(1)} %get-tuple-element.69), channel_id=1, source_target_pairs={{1,0},{2,1},{3,2},{4,3},{5,4},{6,5},{7,6},{9,8},{10,9},{11,10},{12... | collective-permute-start | bytes 1572872 | tf_op jit(solution)/shard_map/ppermute | solution.py:22
  7.7 1.0 fusion.41
  8.7 0.0 copy-start.4
  8.7 0.0 copy-start.5
  8.7 0.0 copy-start.3
  8.7 1.0 fusion.42
  9.7 0.0 copy-start.6
  9.7 1.0 fusion.43
  10.8 0.2 copy.125
  11.0 0.1 sub.62
  11.1 0.1 div.16
  11.2 0.2 copy.155
  11.4 0.1 bitcast_bitcast_fusion.1
  11.5 0.0 slice-start
  11.5 0.0 copy-start.2
  11.5 0.2 copy.119
  11.7 0.6 copy.123
  12.4 0.1 select_reduce_fusion
  12.5 0.1 fusion.45
  12.6 0.1 fusion.37
  12.7 0.2 collective-permute-done
  12.9 1.4 %collective-permute-done.1 = f32[1,1,8,128,128]{4,3,2,1,0:T(8,128)} collective-permute-done((f32[1,1,8,128,128]{4,3,2,1,0:T(8,128)S(1)}, f32[1,1,8,128,128]{4,3,2,1,0:T(8,128)}, u32[]{:S(2)}, u32[]{:S(2)}) %collective-permute-start.1) | collective-permute-done | bytes 524320 | tf_op jit(solution)/shard_map/ppermute | solution.py:22
  14.4 1.5 %maximum_bitcast_fusion = f32[4,8,128,128]{3,2,1,0:T(8,128)S(1)} fusion(f32[1,1,8,128,128]{4,3,2,1,0:T(8,128)} %collective-permute-done.1, f32[1,2,8,128,128]{4,3,2,1,0:T(8,128)S(1)} %copy-done.2, f32[1,1,8,128,128]{4,3,2,1,0:T(8,128)} %collective-permute-done), kind=kLoop, calls=%fused_computation.13 | loop fusion | flops 1048576 | bytes 4194304
  15.9 2.3 %fusion.9 = f32[16,128,128]{2,0,1:T(8,128)S(1)} fusion(f32[16,32]{1,0:T(8,128)S(1)} %select_reduce_fusion, f32[4,8,128,128]{3,2,1,0:T(8,128)S(1)} %maximum_bitcast_fusion), kind=kOutput, calls=%fused_computation.10 | convolution fusion | flops 100663296 | bytes 3147776 | tf_op jit(solution)/shard_map/while/body/eval_jaxpr/dot_general | solution.py:120
  18.1 0.3 maximum_bitcast_fusion.1
  18.4 4.6 %fusion.12 = f32[2,128,32,128]{3,1,0,2:T(8,128)S(1)} fusion(f32[32,128,128,1]{2,0,1,3:T(8,128)S(1)} %maximum_bitcast_fusion.1, f32[128,1,128]{0,2,1:T(8,128)S(1)} %get-tuple-element.77, f32[128,1,128]{0,2,1:T(8,128)S(1)} %get-tuple-element.78), kind=kOutput, calls=%fused_computation.15 | convolution fusion | flops 1610645504 | bytes 6422528 | tf_op jit(solution)/shard_map/while/body/eval_jaxpr/tab,bpl->tpla/dot_general | solution.py:68
  23.1 7.6 %fusion.6 = f32[32,128,512]{2,1,0:T(8,128)S(1)} fusion(f32[512,2,128,1]{2,0,1,3:T(8,128)S(1)} %bitcast.146, f32[2,128,32,128]{3,1,0,2:T(8,128)S(1)} %fusion.12), kind=kOutput, calls=%fused_computation.6 | convolution fusion | flops 6442450944 | bytes 13107200 | tf_op jit(solution)/shard_map/while/body/eval_jaxpr/tpla,opa->tlo/dot_general | solution.py:70
  30.7 3.2 %copy-done.1 = f32[32,128,512]{2,1,0:T(8,128)} copy-done((f32[32,128,512]{2,1,0:T(8,128)}, f32[32,128,512]{2,1,0:T(8,128)S(1)}, u32[]{:S(2)}) %copy-start.1) | copy-done | bytes 8388632
  34.0 0.1 slice.256
  34.1 0.1 slice.253
  34.1 0.1 slice.250
  34.2 0.1 slice.247
  34.3 0.1 reverse.8
  34.4 0.1 slice_bitcast_fusion.10
  34.5 0.1 reverse.11
  34.7 0.1 slice_bitcast_fusion.7
  34.7 0.1 reverse.10
  34.9 0.1 slice_bitcast_fusion.8
  35.0 0.1 reverse.9
  35.1 0.1 slice_bitcast_fusion.9
  35.2 0.1 add_bitcast_fusion
  35.3 0.1 subtract_bitcast_fusion
  35.4 4.6 %subtract_select_fusion = (f32[16,128,256]{2,1,0:T(8,128)S(1)}, f32[16,128,256]{2,1,0:T(8,128)S(1)}) fusion(f32[32,128,512]{2,1,0:T(8,128)} %copy-done.1, f32[16,256]{1,0:T(8,128)S(1)} %subtract_bitcast_fusion, pred[128]{0:T(512)(128)(4,1)S(1)} %iota_compare_fusion.1, f32[16,256]{1,0:T(8,128)S(1)} %add_bitcast_fusion), kind=kLoop, calls=%fused_computation.18 | loop fusion | flops 4194304 | bytes 12615808 | tf_op jit(solution)/shard_map/while/body/eval_jaxpr/jit(_where)/select_n | solution.py:96
  40.0 7.0 %fusion = f32[512,16,128]{2,0,1:T(8,128)S(1)} fusion(f32[16,128,256]{2,1,0:T(8,128)S(1)} %get-tuple-element.57, f32[16,128,256]{2,1,0:T(8,128)S(1)} %get-tuple-element.56, f32[256,256]{0,1:T(8,128)S(1)} %fusion.42, f32[256,256]{0,1:T(8,128)S(1)} %fusion.41, f32[256,256]{0,1:T(8,128)S(1)} %fusion.43), kind=kOutput, calls=%fused_computation | convolution fusion | flops 3223060480 | bytes 9175040 | tf_op jit(solution)/shard_map/while/body/eval_jaxpr/tlq,oq->tol/dot_general | solution.py:104
  47.0 1.9 %convolution_bitcast_fusion = f32[2,8,256,256]{2,3,1,0:T(8,128)S(1)} fusion(f32[2,8,256,128,2]{3,2,4,1,0:T(8,128)S(1)} %bitcast.143, f32[1,128,256]{1,2,0:T(8,128)S(1)} %get-tuple-element.75, f32[1,128,256]{1,2,0:T(8,128)S(1)} %get-tuple-element.74), kind=kOutput, calls=%fused_computation.8 | convolution fusion | flops 1610743808 | bytes 8650752 | tf_op jit(solution)/shard_map/while/body/eval_jaxpr/tpml,pln->tmn/dot_general | solution.py:106
  49.0 0.4 fusion.53
  49.4 0.3 pad_add_fusion
  49.7 0.1 fusion.54
  49.9 0.3 copy.152
  50.2 0.3 copy.153
  50.5 0.2 pad_add_fusion.1
  50.8 3.9 %collective-permute-start.2 = (f32[1,64,1024]{2,1,0:T(8,128)S(1)}, f32[1,64,1024]{2,1,0:T(8,128)S(1)}, u32[]{:S(2)}, u32[]{:S(2)}) collective-permute-start(f32[1,64,1024]{2,1,0:T(8,128)S(1)} %get-tuple-element.67), channel_id=1, source_target_pairs={{0,1},{1,2},{2,3},{3,4},{4,5},{5,6},{6,7},{8,9},{9,10},{10,11},{11... | collective-permute-start | bytes 786440 | tf_op jit(solution)/shard_map/ppermute | solution.py:32
  54.7 2.0 %collective-permute-start.3 = (f32[1,64,1024]{2,1,0:T(8,128)S(1)}, f32[1,64,1024]{2,1,0:T(8,128)S(1)}, u32[]{:S(2)}, u32[]{:S(2)}) collective-permute-start(f32[1,64,1024]{2,1,0:T(8,128)S(1)} %get-tuple-element.66), channel_id=1, source_target_pairs={{1,0},{2,1},{3,2},{4,3},{5,4},{6,5},{7,6},{9,8},{10,9},{11,10},{12... | collective-permute-start | bytes 786440 | tf_op jit(solution)/shard_map/ppermute | solution.py:32
  56.6 0.1 slice.267
  56.7 2.0 %collective-permute-done.2 = f32[1,64,1024]{2,1,0:T(8,128)S(1)} collective-permute-done((f32[1,64,1024]{2,1,0:T(8,128)S(1)}, f32[1,64,1024]{2,1,0:T(8,128)S(1)}, u32[]{:S(2)}, u32[]{:S(2)}) %collective-permute-start.2) | collective-permute-done | bytes 262176 | tf_op jit(solution)/shard_map/ppermute | solution.py:32
  58.8 1.7 %collective-permute-done.3 = f32[1,64,1024]{2,1,0:T(8,128)S(1)} collective-permute-done((f32[1,64,1024]{2,1,0:T(8,128)S(1)}, f32[1,64,1024]{2,1,0:T(8,128)S(1)}, u32[]{:S(2)}, u32[]{:S(2)}) %collective-permute-start.3) | collective-permute-done | bytes 262176 | tf_op jit(solution)/shard_map/ppermute | solution.py:32
  60.5 0.1 fusion.25
  60.6 40.0 %all_to_all.5 = f32[1,32,8,1024]{3,2,0,1:T(8,128)S(1)} all-to-all(f32[1,32,8,1024]{3,2,0,1:T(8,128)S(1)} %bitcast.142), channel_id=1, replica_groups=mesh['wave'=32,'tile'=8] {'wave'}, dimensions={1} | all-to-all | bytes 2097152 | tf_op jit(solution)/shard_map/all_to_all | solution.py:176
  100.5 0.0 copy-done
  100.5 1.2 %convolution_bitcast_fusion.1 = f32[3,8,1024]{2,0,1:T(4,128)S(1)} fusion(f32[1,32,8,1024]{3,2,0,1:T(8,128)S(1)} %all_to_all.5, f32[3,32]{1,0:T(4,128)S(1)} %copy-done), kind=kOutput, calls=%fused_computation.20 | convolution fusion | flops 9437184 | bytes 1147264 | tf_op jit(solution)/shard_map/csi,isrx->crx/dot_general | solution.py:179
  101.8 0.7 copy.139
  (29 shorter events, 0.3 us)
Async XLA Ops:
  0.0 100.5 %copy-start = (f32[3,32]{1,0:T(4,128)S(1)}, f32[3,32]{1,0:T(4,128)}, u32[]{:S(2)}) copy-start(f32[3,32]{1,0:T(4,128)} %param.13) | copy-start | bytes 1156
  2.1 10.8 %collective-permute-start = (f32[1,1,8,128,128]{4,3,2,1,0:T(8,128)}, f32[1,1,8,128,128]{4,3,2,1,0:T(8,128)}, u32[]{:S(2)}, u32[]{:S(2)}) collective-permute-start(f32[1,1,8,128,128]{4,3,2,1,0:T(8,128)} %get-tuple-element.68), channel_id=1, source_target_pairs={{0,1},{1,2},{2,3},{3,4},{4,5},{5,6},{6,7},{8,9},{9,10},{10,11},{11... | collective-permute-start | bytes 1572872 | tf_op jit(solution)/shard_map/ppermute | solution.py:20
  4.0 10.3 %collective-permute-start.1 = (f32[1,1,8,128,128]{4,3,2,1,0:T(8,128)S(1)}, f32[1,1,8,128,128]{4,3,2,1,0:T(8,128)}, u32[]{:S(2)}, u32[]{:S(2)}) collective-permute-start(f32[1,1,8,128,128]{4,3,2,1,0:T(8,128)S(1)} %get-tuple-element.69), channel_id=1, source_target_pairs={{1,0},{2,1},{3,2},{4,3},{5,4},{6,5},{7,6},{9,8},{10,9},{11,10},{12... | collective-permute-start | bytes 1572872 | tf_op jit(solution)/shard_map/ppermute | solution.py:22
  8.7 2.3 %copy-start.4 = (s32[2,8,4]{1,2,0:T(4,128)S(1)}, s32[2,8,4]{1,2,0:T(4,128)}, u32[]{:S(2)}) copy-start(s32[2,8,4]{1,2,0:T(4,128)} %param.11) | copy-start | bytes 772
  8.7 2.4 %copy-start.5 = (s32[2,8,4]{1,2,0:T(4,128)S(1)}, s32[2,8,4]{1,2,0:T(4,128)}, u32[]{:S(2)}) copy-start(s32[2,8,4]{1,2,0:T(4,128)} %param.12) | copy-start | bytes 772
  8.7 2.5 %copy-start.3 = (f32[1,256,1024]{2,1,0:T(8,128)S(1)}, f32[1,256,1024]{2,1,0:T(8,128)}, u32[]{:S(2)}) copy-start(f32[1,256,1024]{2,1,0:T(8,128)} %param.9) | copy-start | bytes 3145732
  9.7 1.7 %copy-start.6 = (f32[256]{0:T(256)}, f32[256]{0:T(256)S(1)}, u32[]{:S(2)}) copy-start(f32[256]{0:T(256)S(1)} %compare_select_fusion) | copy-start | bytes 3076
  11.5 1.0 slice-start
  11.5 1.1 %copy-start.7 = (f32[256]{0:T(256)S(1)}, f32[256]{0:T(256)}, u32[]{:S(2)}) copy-start(f32[256]{0:T(256)} %copy-done.6) | copy-start | bytes 3076
  11.5 2.8 %copy-start.2 = (f32[1,2,8,128,128]{4,3,2,1,0:T(8,128)S(1)}, f32[1,2,8,128,128]{4,3,2,1,0:T(8,128)}, u32[]{:S(2)}) copy-start(f32[1,2,8,128,128]{4,3,2,1,0:T(8,128)} %param.10) | copy-start | bytes 3145732
  30.7 3.2 %copy-start.1 = (f32[32,128,512]{2,1,0:T(8,128)}, f32[32,128,512]{2,1,0:T(8,128)S(1)}, u32[]{:S(2)}) copy-start(f32[32,128,512]{2,1,0:T(8,128)S(1)} %fusion.6) | copy-start | bytes 25165828
  50.8 8.0 %collective-permute-start.2 = (f32[1,64,1024]{2,1,0:T(8,128)S(1)}, f32[1,64,1024]{2,1,0:T(8,128)S(1)}, u32[]{:S(2)}, u32[]{:S(2)}) collective-permute-start(f32[1,64,1024]{2,1,0:T(8,128)S(1)} %get-tuple-element.67), channel_id=1, source_target_pairs={{0,1},{1,2},{2,3},{3,4},{4,5},{5,6},{6,7},{8,9},{9,10},{10,11},{11... | collective-permute-start | bytes 786440 | tf_op jit(solution)/shard_map/ppermute | solution.py:32
  54.7 5.8 %collective-permute-start.3 = (f32[1,64,1024]{2,1,0:T(8,128)S(1)}, f32[1,64,1024]{2,1,0:T(8,128)S(1)}, u32[]{:S(2)}, u32[]{:S(2)}) collective-permute-start(f32[1,64,1024]{2,1,0:T(8,128)S(1)} %get-tuple-element.66), channel_id=1, source_target_pairs={{1,0},{2,1},{3,2},{4,3},{5,4},{6,5},{7,6},{9,8},{10,9},{11,10},{12... | collective-permute-start | bytes 786440 | tf_op jit(solution)/shard_map/ppermute | solution.py:32

commit v5 on v4

--- a/solution.py
+++ b/solution.py
@@ -106,6 +106,16 @@
     return jnp.einsum("tpml,pln->tmn", both, last, precision=high)
 
 
+def column_sum(circular, side, width):
+    tile_cols = circular.shape[0]
+    margin = side // 2
+    left_half = jnp.pad(circular[..., :side], ((0, 1), (0, 0), (0, 0)))
+    right_half = jnp.pad(circular[..., side:], ((1, 0), (0, 0), (0, 0)))
+    columns = (left_half + right_half).transpose(1, 0, 2)
+    columns = columns.reshape(circular.shape[1], (tile_cols + 1) * side)
+    return columns[:, margin : margin + width]
+
+
 def blur_wave(scene_plane, extended_plane, mixing, tables):
     first, rows_fwd, rows_inv, last = tables
     slots, tile_cols, side = (
@@ -117,27 +127,34 @@
     tiles = tile_rows * tile_cols
     width = scene_plane.shape[1]
     margin = side // 2
-    psf_set = jnp.dot(mixing, extended_plane.reshape(slots, side * side), precision=highest)
-    psf_set = psf_set.reshape(tiles, side, side)
+    length = 2 * side
     tile_set = (
         scene_plane.reshape(tile_rows, side, tile_cols, side)
         .transpose(0, 2, 1, 3)
         .reshape(tiles, side, side)
     )
-    spec_real, spec_imag = forward(jnp.concatenate([tile_set, psf_set]), first, rows_fwd)
-    prod_real, prod_imag = product(
-        (spec_real[:tiles], spec_imag[:tiles]), (spec_real[tiles:], spec_imag[tiles:])
-    )
-    circular = inverse(prod_real, prod_imag, rows_inv, last)
-    circular = circular.reshape(tile_rows, tile_cols, 2 * side, 2 * side)
-    left_half = jnp.pad(circular[..., :side], ((0, 0), (0, 1), (0, 0), (0, 0)))
-    right_half = jnp.pad(circular[..., side:], ((0, 0), (1, 0), (0, 0), (0, 0)))
-    columns = (left_half + right_half).transpose(0, 2, 1, 3)
-    columns = columns.reshape(tile_rows, 2 * side, (tile_cols + 1) * side)
-    columns = columns[:, :, margin : margin + tile_cols * side]
-    top_half = jnp.pad(columns[:, :side], ((0, 1), (0, 0), (0, 0)))
-    bottom_half = jnp.pad(columns[:, side:], ((1, 0), (0, 0), (0, 0)))
-    return (top_half + bottom_half).reshape((tile_rows + 1) * side, width)
+    scene_spec = forward(tile_set, first, rows_fwd)
+    psf_set = jnp.dot(mixing, extended_plane.reshape(slots, side * side), precision=highest)
+    psf_spec = forward(psf_set.reshape(tiles, side, side), first, rows_fwd)
+    prod_real, prod_imag = product(scene_spec, psf_spec)
+    stacked = jnp.concatenate([prod_real, prod_imag], axis=-1)
+    both = jnp.einsum("tlq,oq->tol", stacked, rows_inv, precision=high)
+    both = both.reshape(tile_rows, tile_cols, 2, length, side)
+
+    def rows_of(row, lo, hi):
+        part = jnp.einsum("cpml,pln->cmn", both[row, :, :, lo:hi], last, precision=high)
+        return column_sum(part, side, width)
+
+    up = rows_of(0, 0, margin)
+    down = rows_of(tile_rows - 1, length - margin, length)
+    strip = tile_rows * side
+    blurred = jnp.zeros((strip, width), jnp.float32)
+    for row in range(tile_rows):
+        lo = margin if row == 0 else 0
+        hi = length - margin if row == tile_rows - 1 else length
+        at = row * side + lo - margin
+        blurred = blurred.at[at : at + hi - lo].add(rows_of(row, lo, hi))
+    return blurred, up, down
 
 
 def per_device(scene, bank, psf_index, psf_weight, response):
@@ -164,10 +181,9 @@
     def one_wave(inputs):
         return blur_wave(inputs[0], inputs[1], mixing, tables)
 
-    summed = lax.map(one_wave, (scene, extended))
-    from_above = from_behind(summed[:, strip + margin :], "tile", 1)
-    from_below = from_behind(summed[:, :margin], "tile", -1)
-    blurred = summed[:, margin : margin + strip]
+    blurred, up, down = lax.map(one_wave, (scene, extended))
+    from_above = from_behind(down, "tile", 1)
+    from_below = from_behind(up, "tile", -1)
     blurred = blurred.at[:, :margin].add(from_above)
     blurred = blurred.at[:, strip - margin :].add(from_below)
     groups = lax.axis_size("wave")

time: 104 us -> 129 us (1.24)
  local copies, waits for them, and re-layouts: 10.1 us -> 36 us
  waiting for transfers between devices: 5.42 us -> 0.01 us
  other arithmetic: 10.4 us -> 15.3 us
    scatter-add x0 -> x4, local copies, waits for them, and re-layouts: none -> 15.9 us  [the longest x1 8.44 us: blur_wave(): blurred = blurred.at[at:at + hi - lo].add(rows_of(row, lo, hi))]
    broadcast_in_dim x0 -> x3, local copies, waits for them, and re-layouts: none -> 3.81 us  [per_device(): blurred, up, down = lax.map(one_wave, (scene, extended))]
    ppermute x2, waiting for transfers between devices: 3.75 us -> 0.01 us  [from_behind(): return lax.ppermute(shard, axis, pairs)]
    transpose x0 -> x2, local copies, waits for them, and re-layouts: none -> 3.06 us  [column_sum(): columns = (left_half + right_half).transpose(1, 0, 2)]
    transpose x0 -> x4, other arithmetic: none -> 2.12 us  [column_sum(): columns = (left_half + right_half).transpose(1, 0, 2)]
    add x2, other arithmetic: 0.46 us -> 2.36 us  [the longest x1 1.24 us: per_device(): blurred = blurred.at[:, strip - margin:].add(from_below)]
    reshape x1 -> x2, local copies, waits for them, and re-layouts: 0.61 us -> 2.13 us  [column_sum(): columns = columns.reshape(circular.shape[1], (tile_cols + 1) * side)]
    ppermute x1, waiting for transfers between devices: 1.44 us -> 0.01 us  [with_halo(): lax.ppermute(head, axis, [((i + 1) % count, i) for i in range(ends)])]
  transfers between devices with their start and end apart: 4 -> 4, of which waited for: 4 -> 0; matrix products, arithmetic and copies ran while one was open for 5% -> 27% of each run, Pallas kernels for 0% -> 0%
where the time goes in v5:
time: 129 us; the launch traced here: 127 us
  blocking collectives  40 us (31%)
  local copies, waits for them, and re-layouts  36 us (28%)
  matrix products  24.7 us (19%)
  other arithmetic  15.3 us (12%)
  starting transfers between devices  10.5 us (8%)
    all_to_all x1, blocking collectives, per_device(): gathered = lax.all_to_all(pieces, 'wave', 1, 1, tiled=True)  40 us
    scatter-add x1, local copies, waits for them, and re-layouts, blur_wave(): blurred = blurred.at[at:at + hi - lo].add(rows_of(row, lo, hi))  8.44 us
    dot_general x2, matrix products, forward(): spec = jnp.einsum('tpla,opa->tlo', packed, rows_fwd, precision=highest)  7.07 us
    dot_general x1, matrix products, blur_wave(): both = jnp.einsum('tlq,oq->tol', stacked, rows_inv, precision=high)  7.05 us
    unnamed x27, local copies, waits for them, and re-layouts  5.03 us
    ppermute x2, starting transfers between devices, from_behind(): return lax.ppermute(shard, axis, pairs)  4.77 us
    select_n x1, other arithmetic, product(): jnp.where(first_column, (low[0] - top[1])[:, None, :], prod_real)  4.56 us
    scatter-add x1, local copies, waits for them, and re-layouts, per_device(): blurred = blurred.at[:, :margin].add(from_above)  4.02 us
  transfers between devices with their start and end apart: 4, of which 0 were waited for; matrix products, arithmetic and copies ran while one was open for 27% of the time, Pallas kernels for 0%

profile of v5, /device:TPU:8, one launch (start us, length us, event | category | flops | bytes accessed | tf_op | source)
XLA Modules:
  0.0 127.1 jit_solution(11698397281610287117)
XLA Ops:
  0.0 2.3 %fusion.65 = (f32[1,1,8,128,128]{4,3,2,1,0:T(8,128)}, f32[1,1,8,128,128]{4,3,2,1,0:T(8,128)}) fusion(f32[1,2,8,128,128]{4,3,2,1,0:T(8,128)} %param.14), kind=kLoop, calls=%fused_computation.128 | loop fusion | bytes 2097152 | tf_op jit(solution)/shard_map/slice | solution.py:17
  2.3 1.9 %collective-permute-start = (f32[1,1,8,128,128]{4,3,2,1,0:T(8,128)}, f32[1,1,8,128,128]{4,3,2,1,0:T(8,128)}, u32[]{:S(2)}, u32[]{:S(2)}) collective-permute-start(f32[1,1,8,128,128]{4,3,2,1,0:T(8,128)} %get-tuple-element.106), channel_id=1, source_target_pairs={{0,1},{1,2},{2,3},{3,4},{4,5},{5,6},{6,7},{8,9},{9,10},{10,11},{11... | collective-permute-start | bytes 1572872 | tf_op jit(solution)/shard_map/ppermute | solution.py:20
  4.3 3.8 %collective-permute-start.1 = (f32[1,1,8,128,128]{4,3,2,1,0:T(8,128)}, f32[1,1,8,128,128]{4,3,2,1,0:T(8,128)}, u32[]{:S(2)}, u32[]{:S(2)}) collective-permute-start(f32[1,1,8,128,128]{4,3,2,1,0:T(8,128)} %get-tuple-element.107), channel_id=1, source_target_pairs={{1,0},{2,1},{3,2},{4,3},{5,4},{6,5},{7,6},{9,8},{10,9},{11,10},{12... | collective-permute-start | bytes 1572872 | tf_op jit(solution)/shard_map/ppermute | solution.py:22
  8.0 1.0 fusion.38
  9.0 1.0 fusion.39
  10.1 0.2 copy.155
  10.4 0.2 copy.212
  10.7 0.2 copy.154
  10.9 0.4 slice-done
  11.2 0.1 fusion.47
  11.3 1.8 %fusion.45 = f32[2,128,16,128]{3,1,0,2:T(8,128)S(1)} fusion(f32[16,128,128,1]{2,1,3,0:T(8,128)S(1)} %bitcast.195, f32[128,1,128]{0,2,1:T(8,128)S(1)} %get-tuple-element.119, f32[128,1,128]{0,2,1:T(8,128)S(1)} %get-tuple-element.120), kind=kOutput, calls=%fused_computation.77 | convolution fusion | flops 805339136 | bytes 3276800 | tf_op jit(solution)/shard_map/while/body/eval_jaxpr/tab,bpl->tpla/dot_general | solution.py:68
  13.2 3.5 %convolution_bitcast_fusion.1 = f32[16,128,512]{2,1,0:T(8,128)S(1)} fusion(f32[512,2,128,1]{2,0,1,3:T(8,128)S(1)} %bitcast.191, f32[2,128,16,128]{3,1,0,2:T(8,128)S(1)} %fusion.45), kind=kOutput, calls=%fused_computation.5 | convolution fusion | flops 3221225472 | bytes 6815744 | tf_op jit(solution)/shard_map/while/body/eval_jaxpr/tpla,opa->tlo/dot_general | solution.py:70
  16.7 1.9 %copy-done.1 = f32[16,128,512]{2,1,0:T(8,128)} copy-done((f32[16,128,512]{2,1,0:T(8,128)}, f32[16,128,512]{2,1,0:T(8,128)S(1)}, u32[]{:S(2)}) %copy-start.1) | copy-done | bytes 4194328
  18.7 0.1 slice.338
  18.8 0.1 slice.332
  18.8 1.0 fusion.44
  19.9 0.1 sub.62
  20.0 0.1 div.16
  20.1 0.3 reverse.10
  20.3 0.1 slice_bitcast_fusion.22
  20.4 0.1 reverse.8
  20.6 0.1 select_reduce_fusion
  20.7 0.1 fusion.37
  20.9 1.5 %maximum_bitcast_fusion = f32[4,8,128,128]{3,2,1,0:T(8,128)S(1)} fusion(f32[1,1,8,128,128]{4,3,2,1,0:T(8,128)} %collective-permute-done.1, f32[1,2,8,128,128]{4,3,2,1,0:T(8,128)S(1)} %copy-done.3, f32[1,1,8,128,128]{4,3,2,1,0:T(8,128)} %collective-permute-done), kind=kLoop, calls=%fused_computation.10 | loop fusion | flops 1048576 | bytes 4194304
  22.3 2.2 %fusion.13 = f32[16,128,128,1]{2,0,1,3:T(8,128)S(1)} fusion(f32[16,32]{1,0:T(8,128)S(1)} %select_reduce_fusion, f32[4,8,128,128]{3,2,1,0:T(8,128)S(1)} %maximum_bitcast_fusion), kind=kOutput, calls=%fused_computation.21 | convolution fusion | flops 100663296 | bytes 3147776 | tf_op jit(solution)/shard_map/while/body/eval_jaxpr/dot_general | solution.py:137
  24.6 2.0 %fusion.24 = f32[2,128,16,128]{3,1,0,2:T(8,128)S(1)} fusion(f32[16,128,128,1]{2,0,1,3:T(8,128)S(1)} %fusion.13, f32[128,1,128]{0,2,1:T(8,128)S(1)} %get-tuple-element.119, f32[128,1,128]{0,2,1:T(8,128)S(1)} %get-tuple-element.120), kind=kOutput, calls=%fused_computation.36 | convolution fusion | flops 805339136 | bytes 3276800 | tf_op jit(solution)/shard_map/while/body/eval_jaxpr/tab,bpl->tpla/dot_general | solution.py:68
  26.6 3.5 %convolution_bitcast_fusion = f32[16,128,512]{2,1,0:T(8,128)S(1)} fusion(f32[512,2,128,1]{2,0,1,3:T(8,128)S(1)} %bitcast.192, f32[2,128,16,128]{3,1,0,2:T(8,128)S(1)} %fusion.24), kind=kOutput, calls=%fused_computation.4 | convolution fusion | flops 3221225472 | bytes 6815744 | tf_op jit(solution)/shard_map/while/body/eval_jaxpr/tpla,opa->tlo/dot_general | solution.py:70
  30.2 2.0 %copy-done.2 = f32[16,128,512]{2,1,0:T(8,128)} copy-done((f32[16,128,512]{2,1,0:T(8,128)}, f32[16,128,512]{2,1,0:T(8,128)S(1)}, u32[]{:S(2)}) %copy-start.2) | copy-done | bytes 4194328
  32.3 0.1 slice.335
  32.3 0.1 reverse.11
  32.5 0.1 slice_bitcast_fusion.21
  32.6 0.3 reverse.9
  32.8 0.1 slice_bitcast_fusion.23
  32.9 0.1 add_bitcast_fusion.4
  33.0 0.1 subtract_bitcast_fusion
  33.1 4.6 %subtract_select_fusion = (f32[16,128,256]{2,1,0:T(8,128)S(1)}, f32[16,128,256]{2,1,0:T(8,128)S(1)}) fusion(f32[16,128,512]{2,1,0:T(8,128)} %copy-done.2, f32[16,128,512]{2,1,0:T(8,128)} %copy-done.1, f32[16,256]{1,0:T(8,128)S(1)} %subtract_bitcast_fusion, pred[128]{0:T(512)(128)(4,1)S(1)} %iota_compare_fusion.1, f32[16,256]{1,0:T(8,128)S(1)} %add_bitcast_fusion.4), kind=kLoop, calls=%fused_computation.14 | loop fusion | flops 4194304 | bytes 12615808 | tf_op jit(solution)/shard_map/while/body/eval_jaxpr/jit(_where)/select_n | solution.py:96
  37.7 7.0 %fusion = f32[512,16,128]{2,0,1:T(8,128)S(1)} fusion(f32[16,128,256]{2,1,0:T(8,128)S(1)} %get-tuple-element.97, f32[16,128,256]{2,1,0:T(8,128)S(1)} %get-tuple-element.96, f32[256,256]{0,1:T(8,128)S(1)} %fusion.39, f32[256,256]{0,1:T(8,128)S(1)} %fusion.38, f32[256,256]{0,1:T(8,128)S(1)} %fusion.44), kind=kOutput, calls=%fused_computation | convolution fusion | flops 3223060480 | bytes 9175040 | tf_op jit(solution)/shard_map/while/body/eval_jaxpr/tlq,oq->tol/dot_general | solution.py:141
  44.7 0.4 convolution_bitcast_fusion.2
  45.1 1.2 convolution_bitcast_fusion.3
  46.4 0.8 fusion.12
  47.2 0.8 fusion.11
  48.1 1.1 copy.204
  49.2 1.9 %slice_bitcast_fusion.8 = f32[1,64,1024]{1,2,0:T(8,128)} fusion(f32[64,1152]{0,1:T(8,128)} %bitcast.202), kind=kLoop, calls=%fused_computation.42 | loop fusion | bytes 524288 | tf_op jit(solution)/shard_map/while/body/jit(dynamic_update_index_in_dim)/broadcast_in_dim | solution.py:184
  51.1 2.6 %collective-permute-start.3 = (f32[1,64,1024]{1,2,0:T(8,128)}, f32[1,64,1024]{1,2,0:T(8,128)}, u32[]{:S(2)}, u32[]{:S(2)}) collective-permute-start(f32[1,64,1024]{1,2,0:T(8,128)} %slice_bitcast_fusion.8), channel_id=1, source_target_pairs={{1,0},{2,1},{3,2},{4,3},{5,4},{6,5},{7,6},{9,8},{10,9},{11,10},{12... | collective-permute-start | bytes 786440 | tf_op jit(solution)/shard_map/ppermute | solution.py:32
  53.7 1.1 fusion.67
  54.8 1.1 copy.202
  55.9 1.9 %slice_bitcast_fusion.11 = f32[1,64,1024]{1,2,0:T(8,128)} fusion(f32[64,1152]{0,1:T(8,128)} %bitcast.203), kind=kLoop, calls=%fused_computation.45 | loop fusion | bytes 524288 | tf_op jit(solution)/shard_map/while/body/jit(dynamic_update_index_in_dim)/broadcast_in_dim | solution.py:184
  57.7 2.2 %collective-permute-start.2 = (f32[1,64,1024]{1,2,0:T(8,128)}, f32[1,64,1024]{1,2,0:T(8,128)}, u32[]{:S(2)}, u32[]{:S(2)}) collective-permute-start(f32[1,64,1024]{1,2,0:T(8,128)} %slice_bitcast_fusion.11), channel_id=1, source_target_pairs={{0,1},{1,2},{2,3},{3,4},{4,5},{5,6},{6,7},{8,9},{9,10},{10,11},{11... | collective-permute-start | bytes 786440 | tf_op jit(solution)/shard_map/ppermute | solution.py:32
  59.9 0.2 fusion.63
  60.1 1.0 add_bitcast_fusion
  61.1 1.5 %copy.172 = f32[192,9,128]{0,2,1:T(8,128)S(1)} copy(f32[192,9,128]{2,0,1:T(8,128)} %add_bitcast_fusion) | data formatting | bytes 1769472 | tf_op jit(solution)/shard_map/while/body/eval_jaxpr/transpose | solution.py:114
  62.6 0.2 fusion.64
  62.8 1.0 add_bitcast_fusion.1
  63.8 1.5 %copy.170 = f32[192,9,128]{0,2,1:T(8,128)S(1)} copy(f32[192,9,128]{2,0,1:T(8,128)} %add_bitcast_fusion.1) | data formatting | bytes 1769472 | tf_op jit(solution)/shard_map/while/body/eval_jaxpr/transpose | solution.py:114
  65.5 1.3 %fusion.16 = f32[1,192,1024]{1,2,0:T(8,128)} fusion(f32[192,1152]{0,1:T(8,128)S(1)} %bitcast.193, f32[192,1024]{0,1:T(8,128)S(1)} %slice.351), kind=kLoop, calls=%fused_computation.27 | loop fusion | flops 196608 | bytes 2359296 | tf_op jit(solution)/shard_map/while/body/jit(dynamic_update_index_in_dim)/broadcast_in_dim | solution.py:184
  66.9 8.4 %scatter-add.17 = f32[1,256,1024]{1,2,0:T(8,128)S(1)} dynamic-update-slice(f32[1,256,1024]{1,2,0:T(8,128)S(1)} %pad_bitcast_fusion, f32[1,192,1024]{1,2,0:T(8,128)} %fusion.16, s32[]{:T(128)} %constant.190.clone.1, s32[]{:T(128)} %constant.207.clone.1, s32[]{:T(128)} %constant.190.clone.1) | dynamic-update-slice | bytes 1572868 | tf_op jit(solution)/shard_map/while/body/eval_jaxpr/scatter-add | solution.py:156
  75.3 1.1 slice_add_fusion.2
  76.4 4.0 %scatter-add.18 = f32[1,256,1024]{1,2,0:T(8,128)S(1)} dynamic-update-slice(f32[1,256,1024]{1,2,0:T(8,128)S(1)} %scatter-add.17, f32[1,64,1024]{1,2,0:T(8,128)S(1)} %slice_add_fusion.2, s32[]{:T(128)} %constant.190.clone.1, s32[]{:T(128)} %constant.190.clone.1, s32[]{:T(128)} %constant.190.clone.1) | dynamic-update-slice | bytes 524292 | tf_op jit(solution)/shard_map/scatter-add | solution.py:187
  80.5 1.2 slice_add_fusion.1
  81.7 3.1 %scatter-add.21 = f32[1,256,1024]{1,2,0:T(8,128)S(1)} dynamic-update-slice(f32[1,256,1024]{1,2,0:T(8,128)S(1)} %scatter-add.18, f32[1,64,1024]{1,2,0:T(8,128)S(1)} %slice_add_fusion.1, s32[]{:T(128)} %constant.190.clone.1, s32[]{:T(128)} %constant.208.clone.1, s32[]{:T(128)} %constant.190.clone.1) | dynamic-update-slice | bytes 524292 | tf_op jit(solution)/shard_map/scatter-add | solution.py:188
  84.8 0.3 copy.179
  85.1 40.0 %all_to_all.5 = f32[1,32,8,1024]{3,2,0,1:T(8,128)S(1)} all-to-all(f32[1,32,8,1024]{3,2,0,1:T(8,128)S(1)} %bitcast.200), channel_id=1, replica_groups=mesh['wave'=32,'tile'=8] {'wave'}, dimensions={1} | all-to-all | bytes 2097152 | tf_op jit(solution)/shard_map/all_to_all | solution.py:192
  125.2 1.2 convolution_bitcast_fusion.4
  126.4 0.7 copy.182
  (48 shorter events, 0.7 us)
Async XLA Ops:
  0.0 125.2 %copy-start = (f32[3,32]{1,0:T(4,128)S(1)}, f32[3,32]{1,0:T(4,128)}, u32[]{:S(2)}) copy-start(f32[3,32]{1,0:T(4,128)} %param.17) | copy-start | bytes 1156
  2.3 18.5 %collective-permute-start = (f32[1,1,8,128,128]{4,3,2,1,0:T(8,128)}, f32[1,1,8,128,128]{4,3,2,1,0:T(8,128)}, u32[]{:S(2)}, u32[]{:S(2)}) collective-permute-start(f32[1,1,8,128,128]{4,3,2,1,0:T(8,128)} %get-tuple-element.106), channel_id=1, source_target_pairs={{0,1},{1,2},{2,3},{3,4},{4,5},{5,6},{6,7},{8,9},{9,10},{10,11},{11... | collective-permute-start | bytes 1572872 | tf_op jit(solution)/shard_map/ppermute | solution.py:20
  4.2 6.1 %copy-start.4 = (f32[1,256,1024]{2,1,0:T(8,128)S(1)}, f32[1,256,1024]{2,1,0:T(8,128)}, u32[]{:S(2)}) copy-start(f32[1,256,1024]{2,1,0:T(8,128)} %param.13) | copy-start | bytes 3145732
  4.3 16.6 %collective-permute-start.1 = (f32[1,1,8,128,128]{4,3,2,1,0:T(8,128)}, f32[1,1,8,128,128]{4,3,2,1,0:T(8,128)}, u32[]{:S(2)}, u32[]{:S(2)}) collective-permute-start(f32[1,1,8,128,128]{4,3,2,1,0:T(8,128)} %get-tuple-element.107), channel_id=1, source_target_pairs={{1,0},{2,1},{3,2},{4,3},{5,4},{6,5},{7,6},{9,8},{10,9},{11,10},{12... | collective-permute-start | bytes 1572872 | tf_op jit(solution)/shard_map/ppermute | solution.py:22
  10.0 0.6 copy-start.7
  10.6 0.7 slice-start
  13.1 6.7 %copy-start.5 = (s32[2,8,4]{1,2,0:T(4,128)S(1)}, s32[2,8,4]{1,2,0:T(4,128)}, u32[]{:S(2)}) copy-start(s32[2,8,4]{1,2,0:T(4,128)} %param.15) | copy-start | bytes 772
  13.1 6.8 %copy-start.6 = (s32[2,8,4]{1,2,0:T(4,128)S(1)}, s32[2,8,4]{1,2,0:T(4,128)}, u32[]{:S(2)}) copy-start(s32[2,8,4]{1,2,0:T(4,128)} %param.16) | copy-start | bytes 772
  13.1 7.6 %copy-start.8 = (f32[256]{0:T(256)S(1)}, f32[256]{0:T(256)}, u32[]{:S(2)}) copy-start(f32[256]{0:T(256)} %copy-done.7) | copy-start | bytes 3076
  13.2 7.7 %copy-start.3 = (f32[1,2,8,128,128]{4,3,2,1,0:T(8,128)S(1)}, f32[1,2,8,128,128]{4,3,2,1,0:T(8,128)}, u32[]{:S(2)}) copy-start(f32[1,2,8,128,128]{4,3,2,1,0:T(8,128)} %param.14) | copy-start | bytes 3145732
  16.7 1.9 %copy-start.1 = (f32[16,128,512]{2,1,0:T(8,128)}, f32[16,128,512]{2,1,0:T(8,128)S(1)}, u32[]{:S(2)}) copy-start(f32[16,128,512]{2,1,0:T(8,128)S(1)} %convolution_bitcast_fusion.1) | copy-start | bytes 12582916
  30.1 2.0 %copy-start.2 = (f32[16,128,512]{2,1,0:T(8,128)}, f32[16,128,512]{2,1,0:T(8,128)S(1)}, u32[]{:S(2)}) copy-start(f32[16,128,512]{2,1,0:T(8,128)S(1)} %convolution_bitcast_fusion) | copy-start | bytes 12582916
  51.1 29.4 %collective-permute-start.3 = (f32[1,64,1024]{1,2,0:T(8,128)}, f32[1,64,1024]{1,2,0:T(8,128)}, u32[]{:S(2)}, u32[]{:S(2)}) collective-permute-start(f32[1,64,1024]{1,2,0:T(8,128)} %slice_bitcast_fusion.8), channel_id=1, source_target_pairs={{1,0},{2,1},{3,2},{4,3},{5,4},{6,5},{7,6},{9,8},{10,9},{11,10},{12... | collective-permute-start | bytes 786440 | tf_op jit(solution)/shard_map/ppermute | solution.py:32
  57.7 17.6 %collective-permute-start.2 = (f32[1,64,1024]{1,2,0:T(8,128)}, f32[1,64,1024]{1,2,0:T(8,128)}, u32[]{:S(2)}, u32[]{:S(2)}) collective-permute-start(f32[1,64,1024]{1,2,0:T(8,128)} %slice_bitcast_fusion.11), channel_id=1, source_target_pairs={{0,1},{1,2},{2,3},{3,4},{4,5},{5,6},{6,7},{8,9},{9,10},{10,11},{11... | collective-permute-start | bytes 786440 | tf_op jit(solution)/shard_map/ppermute | solution.py:32

commit v6 on v5

--- a/solution.py
+++ b/solution.py
@@ -148,12 +148,13 @@
     up = rows_of(0, 0, margin)
     down = rows_of(tile_rows - 1, length - margin, length)
     strip = tile_rows * side
-    blurred = jnp.zeros((strip, width), jnp.float32)
+    bands = []
     for row in range(tile_rows):
         lo = margin if row == 0 else 0
         hi = length - margin if row == tile_rows - 1 else length
         at = row * side + lo - margin
-        blurred = blurred.at[at : at + hi - lo].add(rows_of(row, lo, hi))
+        bands.append(jnp.pad(rows_of(row, lo, hi), ((at, strip - at - (hi - lo)), (0, 0))))
+    blurred = sum(bands[1:], bands[0])
     return blurred, up, down
 
 
@@ -184,8 +185,11 @@
     blurred, up, down = lax.map(one_wave, (scene, extended))
     from_above = from_behind(down, "tile", 1)
     from_below = from_behind(up, "tile", -1)
-    blurred = blurred.at[:, :margin].add(from_above)
-    blurred = blurred.at[:, strip - margin :].add(from_below)
+    blurred = (
+        blurred
+        + jnp.pad(from_above, ((0, 0), (0, strip - margin), (0, 0)))
+        + jnp.pad(from_below, ((0, 0), (strip - margin, 0), (0, 0)))
+    )
     groups = lax.axis_size("wave")
     width = blurred.shape[-1]
     pieces = blurred.reshape(wave_count, groups, strip // groups, width)

time: 129 us -> 109 us (0.84)
  local copies, waits for them, and re-layouts: 36 us -> 15.9 us
  waiting for transfers between devices: 0.01 us -> 4.36 us
  other arithmetic: 15.3 us -> 11.4 us
    scatter-add x4 -> x0, local copies, waits for them, and re-layouts: 15.9 us -> none  [the longest x1 8.44 us: blur_wave(): blurred = blurred.at[at:at + hi - lo].add(rows_of(row, lo, hi))]
    ppermute x2, waiting for transfers between devices: 0.01 us -> 4.35 us  [from_behind(): return lax.ppermute(shard, axis, pairs)]
    transpose x2, local copies, waits for them, and re-layouts: 3.06 us -> 0.73 us  [column_sum(): columns = (left_half + right_half).transpose(1, 0, 2)]
    broadcast_in_dim x3 -> x2, local copies, waits for them, and re-layouts: 3.81 us -> 1.68 us  [per_device(): blurred, up, down = lax.map(one_wave, (scene, extended))]
    transpose x4, other arithmetic: 2.12 us -> 0.25 us  [column_sum(): columns = (left_half + right_half).transpose(1, 0, 2)]
    reshape x2, local copies, waits for them, and re-layouts: 2.13 us -> 0.47 us  [column_sum(): columns = columns.reshape(circular.shape[1], (tile_cols + 1) * side)]
    broadcast_in_dim x1 -> x0, other arithmetic: 1.34 us -> none  [per_device(): blurred, up, down = lax.map(one_wave, (scene, extended))]
    unnamed x27 -> x31, local copies, waits for them, and re-layouts: 5.03 us -> 6.32 us
  transfers between devices with their start and end apart: 4 -> 4, of which waited for: 0 -> 2; matrix products, arithmetic and copies ran while one was open for 27% -> 12% of each run, Pallas kernels for 0% -> 0%
where the time goes in v6:
time: 109 us; the launch traced here: 108 us
  blocking collectives  40 us (37%)
  matrix products  23.9 us (22%)
  local copies, waits for them, and re-layouts  15.9 us (15%)
  starting transfers between devices  11.5 us (11%)
  other arithmetic  11.4 us (10%)
  waiting for transfers between devices  4.36 us (4%)
    all_to_all x1, blocking collectives, per_device(): gathered = lax.all_to_all(pieces, 'wave', 1, 1, tiled=True)  40 us
    dot_general x2, matrix products, forward(): spec = jnp.einsum('tpla,opa->tlo', packed, rows_fwd, precision=highest)  7.06 us
    dot_general x1, matrix products, blur_wave(): both = jnp.einsum('tlq,oq->tol', stacked, rows_inv, precision=high)  7.05 us
    unnamed x31, local copies, waits for them, and re-layouts  6.32 us
    ppermute x2, starting transfers between devices, from_behind(): return lax.ppermute(shard, axis, pairs)  5.8 us
    select_n x1, other arithmetic, product(): jnp.where(first_column, (low[0] - top[1])[:, None, :], prod_real)  4.56 us
    ppermute x2, waiting for transfers between devices, from_behind(): return lax.ppermute(shard, axis, pairs)  4.35 us
    dot_general x2, matrix products, forward(): packed = jnp.einsum('tab,bpl->tpla', blocks, first, precision=highest)  3.82 us
  transfers between devices with their start and end apart: 4, of which 2 were waited for; matrix products, arithmetic and copies ran while one was open for 12% of the time, Pallas kernels for 0%

profile of v6, /device:TPU:8, one launch (start us, length us, event | category | flops | bytes accessed | tf_op | source)
XLA Modules:
  0.0 107.6 jit_solution(5652793039839265339)
XLA Ops:
  0.0 2.3 %fusion.65 = (f32[1,1,8,128,128]{4,3,2,1,0:T(8,128)}, f32[1,1,8,128,128]{4,3,2,1,0:T(8,128)}) fusion(f32[1,2,8,128,128]{4,3,2,1,0:T(8,128)} %param.6), kind=kLoop, calls=%fused_computation.125 | loop fusion | bytes 2097152 | tf_op jit(solution)/shard_map/slice | solution.py:17
  2.3 1.9 %collective-permute-start = (f32[1,1,8,128,128]{4,3,2,1,0:T(8,128)}, f32[1,1,8,128,128]{4,3,2,1,0:T(8,128)}, u32[]{:S(2)}, u32[]{:S(2)}) collective-permute-start(f32[1,1,8,128,128]{4,3,2,1,0:T(8,128)} %get-tuple-element.48), channel_id=1, source_target_pairs={{0,1},{1,2},{2,3},{3,4},{4,5},{5,6},{6,7},{8,9},{9,10},{10,11},{11... | collective-permute-start | bytes 1572872 | tf_op jit(solution)/shard_map/ppermute | solution.py:20
  4.3 3.8 %collective-permute-start.1 = (f32[1,1,8,128,128]{4,3,2,1,0:T(8,128)}, f32[1,1,8,128,128]{4,3,2,1,0:T(8,128)}, u32[]{:S(2)}, u32[]{:S(2)}) collective-permute-start(f32[1,1,8,128,128]{4,3,2,1,0:T(8,128)} %get-tuple-element.49), channel_id=1, source_target_pairs={{1,0},{2,1},{3,2},{4,3},{5,4},{6,5},{7,6},{9,8},{10,9},{11,10},{12... | collective-permute-start | bytes 1572872 | tf_op jit(solution)/shard_map/ppermute | solution.py:22
  8.0 1.0 fusion.38
  9.0 1.0 fusion.39
  10.1 0.2 copy.155
  10.3 0.2 copy.212
  10.7 0.2 copy.154
  10.9 0.4 slice-done
  11.2 0.1 fusion.47
  11.3 1.8 %fusion.45 = f32[2,128,16,128]{3,1,0,2:T(8,128)S(1)} fusion(f32[16,128,128,1]{2,1,3,0:T(8,128)S(1)} %bitcast.195, f32[128,1,128]{0,2,1:T(8,128)S(1)} %get-tuple-element.61, f32[128,1,128]{0,2,1:T(8,128)S(1)} %get-tuple-element.62), kind=kOutput, calls=%fused_computation.74 | convolution fusion | flops 805339136 | bytes 3276800 | tf_op jit(solution)/shard_map/while/body/eval_jaxpr/tab,bpl->tpla/dot_general | solution.py:68
  13.2 3.5 %convolution_bitcast_fusion.1 = f32[16,128,512]{2,1,0:T(8,128)S(1)} fusion(f32[512,2,128,1]{2,0,1,3:T(8,128)S(1)} %bitcast.191, f32[2,128,16,128]{3,1,0,2:T(8,128)S(1)} %fusion.45), kind=kOutput, calls=%fused_computation.5 | convolution fusion | flops 3221225472 | bytes 6815744 | tf_op jit(solution)/shard_map/while/body/eval_jaxpr/tpla,opa->tlo/dot_general | solution.py:70
  16.7 1.9 %copy-done.1 = f32[16,128,512]{2,1,0:T(8,128)} copy-done((f32[16,128,512]{2,1,0:T(8,128)}, f32[16,128,512]{2,1,0:T(8,128)S(1)}, u32[]{:S(2)}) %copy-start.1) | copy-done | bytes 4194328
  18.7 0.1 slice.238
  18.8 0.1 slice.232
  18.8 1.0 fusion.44
  19.9 0.1 sub.62
  20.0 0.1 div.16
  20.0 0.3 reverse.10
  20.3 0.1 slice_bitcast_fusion.22
  20.4 0.1 reverse.8
  20.5 0.1 select_reduce_fusion
  20.6 0.1 slice_bitcast_fusion.24
  20.7 0.1 fusion.37
  20.8 1.5 %maximum_bitcast_fusion = f32[4,8,128,128]{3,2,1,0:T(8,128)S(1)} fusion(f32[1,1,8,128,128]{4,3,2,1,0:T(8,128)} %collective-permute-done.1, f32[1,2,8,128,128]{4,3,2,1,0:T(8,128)S(1)} %copy-done.3, f32[1,1,8,128,128]{4,3,2,1,0:T(8,128)} %collective-permute-done), kind=kLoop, calls=%fused_computation.10 | loop fusion | flops 1048576 | bytes 4194304
  22.3 2.2 %fusion.13 = f32[16,128,128,1]{2,0,1,3:T(8,128)S(1)} fusion(f32[16,32]{1,0:T(8,128)S(1)} %select_reduce_fusion, f32[4,8,128,128]{3,2,1,0:T(8,128)S(1)} %maximum_bitcast_fusion), kind=kOutput, calls=%fused_computation.21 | convolution fusion | flops 100663296 | bytes 3147776 | tf_op jit(solution)/shard_map/while/body/eval_jaxpr/dot_general | solution.py:137
  24.6 2.0 %fusion.24 = f32[2,128,16,128]{3,1,0,2:T(8,128)S(1)} fusion(f32[16,128,128,1]{2,0,1,3:T(8,128)S(1)} %fusion.13, f32[128,1,128]{0,2,1:T(8,128)S(1)} %get-tuple-element.61, f32[128,1,128]{0,2,1:T(8,128)S(1)} %get-tuple-element.62), kind=kOutput, calls=%fused_computation.36 | convolution fusion | flops 805339136 | bytes 3276800 | tf_op jit(solution)/shard_map/while/body/eval_jaxpr/tab,bpl->tpla/dot_general | solution.py:68
  26.6 3.5 %convolution_bitcast_fusion = f32[16,128,512]{2,1,0:T(8,128)S(1)} fusion(f32[512,2,128,1]{2,0,1,3:T(8,128)S(1)} %bitcast.192, f32[2,128,16,128]{3,1,0,2:T(8,128)S(1)} %fusion.24), kind=kOutput, calls=%fused_computation.4 | convolution fusion | flops 3221225472 | bytes 6815744 | tf_op jit(solution)/shard_map/while/body/eval_jaxpr/tpla,opa->tlo/dot_general | solution.py:70
  30.1 2.0 %copy-done.2 = f32[16,128,512]{2,1,0:T(8,128)} copy-done((f32[16,128,512]{2,1,0:T(8,128)}, f32[16,128,512]{2,1,0:T(8,128)S(1)}, u32[]{:S(2)}) %copy-start.2) | copy-done | bytes 4194328
  32.2 0.1 slice.241
  32.3 0.1 slice.235
  32.3 0.1 reverse.11
  32.5 0.1 slice_bitcast_fusion.21
  32.6 0.3 reverse.9
  32.8 0.1 slice_bitcast_fusion.23
  32.9 0.1 add_bitcast_fusion.4
  33.0 0.1 subtract_bitcast_fusion
  33.1 4.6 %subtract_select_fusion = (f32[16,128,256]{2,1,0:T(8,128)S(1)}, f32[16,128,256]{2,1,0:T(8,128)S(1)}) fusion(f32[16,128,512]{2,1,0:T(8,128)} %copy-done.2, f32[16,128,512]{2,1,0:T(8,128)} %copy-done.1, f32[16,256]{1,0:T(8,128)S(1)} %subtract_bitcast_fusion, pred[128]{0:T(512)(128)(4,1)S(1)} %iota_compare_fusion.1, f32[16,256]{1,0:T(8,128)S(1)} %add_bitcast_fusion.4), kind=kLoop, calls=%fused_computation.14 | loop fusion | flops 4194304 | bytes 12615808 | tf_op jit(solution)/shard_map/while/body/eval_jaxpr/jit(_where)/select_n | solution.py:96
  37.7 7.0 %fusion = f32[512,16,128]{2,0,1:T(8,128)S(1)} fusion(f32[16,128,256]{2,1,0:T(8,128)S(1)} %get-tuple-element.26, f32[16,128,256]{2,1,0:T(8,128)S(1)} %get-tuple-element.25, f32[256,256]{0,1:T(8,128)S(1)} %fusion.39, f32[256,256]{0,1:T(8,128)S(1)} %fusion.38, f32[256,256]{0,1:T(8,128)S(1)} %fusion.44), kind=kOutput, calls=%fused_computation | convolution fusion | flops 3223060480 | bytes 9175040 | tf_op jit(solution)/shard_map/while/body/eval_jaxpr/tlq,oq->tol/dot_general | solution.py:141
  44.7 0.8 fusion.11
  45.6 0.8 fusion.12
  46.4 0.4 convolution_bitcast_fusion.3
  46.8 0.4 convolution_bitcast_fusion.2
  47.3 0.2 fusion.63
  47.4 1.4 %fusion.64 = (f32[8,192,128]{2,1,0:T(8,128)}, f32[8,192,128]{2,1,0:T(8,128)}) fusion(f32[8,192,256]{2,1,0:T(8,128)S(1)} %fusion.12), kind=kLoop, calls=%fused_computation.124 | loop fusion | bytes 3145728 | tf_op jit(solution)/shard_map/while/body/eval_jaxpr/slice | solution.py:112
  48.9 0.2 copy.202
  49.1 0.8 slice_bitcast_fusion.11
  49.9 1.9 %collective-permute-start.2 = (f32[1,64,1024]{1,2,0:T(8,128)}, f32[1,64,1024]{1,2,0:T(8,128)}, u32[]{:S(2)}, u32[]{:S(2)}) collective-permute-start(f32[1,64,1024]{1,2,0:T(8,128)} %slice_bitcast_fusion.11), channel_id=1, source_target_pairs={{0,1},{1,2},{2,3},{3,4},{4,5},{5,6},{6,7},{8,9},{9,10},{10,11},{11... | collective-permute-start | bytes 786440 | tf_op jit(solution)/shard_map/ppermute | solution.py:32
  52.0 0.2 copy.204
  52.2 0.8 slice_bitcast_fusion.8
  53.0 3.9 %collective-permute-start.3 = (f32[1,64,1024]{1,2,0:T(8,128)}, f32[1,64,1024]{1,2,0:T(8,128)}, u32[]{:S(2)}, u32[]{:S(2)}) collective-permute-start(f32[1,64,1024]{1,2,0:T(8,128)} %slice_bitcast_fusion.8), channel_id=1, source_target_pairs={{1,0},{2,1},{3,2},{4,3},{5,4},{6,5},{7,6},{9,8},{10,9},{11,10},{12... | collective-permute-start | bytes 786440 | tf_op jit(solution)/shard_map/ppermute | solution.py:32
  56.9 0.1 add_bitcast_fusion.1
  57.0 0.4 copy.170
  57.5 1.0 copy-done.4
  58.5 0.2 copy-done.5
  58.8 0.1 add_bitcast_fusion
  58.9 0.4 copy.172
  59.3 1.4 %collective-permute-done.2 = f32[1,64,1024]{1,2,0:T(8,128)} collective-permute-done((f32[1,64,1024]{1,2,0:T(8,128)}, f32[1,64,1024]{1,2,0:T(8,128)}, u32[]{:S(2)}, u32[]{:S(2)}) %collective-permute-start.2) | collective-permute-done | bytes 262176 | tf_op jit(solution)/shard_map/ppermute | solution.py:32
  60.7 2.9 %collective-permute-done.3 = f32[1,64,1024]{1,2,0:T(8,128)} collective-permute-done((f32[1,64,1024]{1,2,0:T(8,128)}, f32[1,64,1024]{1,2,0:T(8,128)}, u32[]{:S(2)}, u32[]{:S(2)}) %collective-permute-start.3) | collective-permute-done | bytes 262176 | tf_op jit(solution)/shard_map/ppermute | solution.py:32
  63.7 1.7 %fusion.23 = f32[1,256,1024]{1,2,0:T(8,128)S(1)} fusion(f32[1,64,1024]{1,2,0:T(8,128)} %collective-permute-done.3, f32[1,64,1024]{1,2,0:T(8,128)} %collective-permute-done.2, f32[192,1024]{0,1:T(8,128)S(1)} %slice.255, f32[192,1024]{0,1:T(8,128)S(1)} %slice.251), kind=kLoop, calls=%fused_computation.35 | loop fusion | flops 786432 | bytes 3145728 | tf_op jit(solution)/shard_map/add | solution.py:189
  65.4 0.3 copy.179
  65.7 40.0 %all_to_all.5 = f32[1,32,8,1024]{3,2,0,1:T(8,128)S(1)} all-to-all(f32[1,32,8,1024]{3,2,0,1:T(8,128)S(1)} %bitcast.200), channel_id=1, replica_groups=mesh['wave'=32,'tile'=8] {'wave'}, dimensions={1} | all-to-all | bytes 2097152 | tf_op jit(solution)/shard_map/all_to_all | solution.py:196
  105.7 1.2 %convolution_bitcast_fusion.4 = f32[3,8,1024]{2,0,1:T(4,128)S(1)} fusion(f32[1,32,8,1024]{3,2,0,1:T(8,128)S(1)} %all_to_all.5, f32[3,32]{1,0:T(4,128)S(1)} %copy-done), kind=kOutput, calls=%fused_computation.24 | convolution fusion | flops 9437184 | bytes 1147264 | tf_op jit(solution)/shard_map/csi,isrx->crx/dot_general | solution.py:199
  106.9 0.7 copy.182
  (47 shorter events, 0.6 us)
Async XLA Ops:
  0.0 105.7 %copy-start = (f32[3,32]{1,0:T(4,128)S(1)}, f32[3,32]{1,0:T(4,128)}, u32[]{:S(2)}) copy-start(f32[3,32]{1,0:T(4,128)} %param.9) | copy-start | bytes 1156
  2.3 18.5 %collective-permute-start = (f32[1,1,8,128,128]{4,3,2,1,0:T(8,128)}, f32[1,1,8,128,128]{4,3,2,1,0:T(8,128)}, u32[]{:S(2)}, u32[]{:S(2)}) collective-permute-start(f32[1,1,8,128,128]{4,3,2,1,0:T(8,128)} %get-tuple-element.48), channel_id=1, source_target_pairs={{0,1},{1,2},{2,3},{3,4},{4,5},{5,6},{6,7},{8,9},{9,10},{10,11},{11... | collective-permute-start | bytes 1572872 | tf_op jit(solution)/shard_map/ppermute | solution.py:20
  4.2 6.1 %copy-start.6 = (f32[1,256,1024]{2,1,0:T(8,128)S(1)}, f32[1,256,1024]{2,1,0:T(8,128)}, u32[]{:S(2)}) copy-start(f32[1,256,1024]{2,1,0:T(8,128)} %param.5) | copy-start | bytes 3145732
  4.3 16.6 %collective-permute-start.1 = (f32[1,1,8,128,128]{4,3,2,1,0:T(8,128)}, f32[1,1,8,128,128]{4,3,2,1,0:T(8,128)}, u32[]{:S(2)}, u32[]{:S(2)}) collective-permute-start(f32[1,1,8,128,128]{4,3,2,1,0:T(8,128)} %get-tuple-element.49), channel_id=1, source_target_pairs={{1,0},{2,1},{3,2},{4,3},{5,4},{6,5},{7,6},{9,8},{10,9},{11,10},{12... | collective-permute-start | bytes 1572872 | tf_op jit(solution)/shard_map/ppermute | solution.py:22
  10.0 0.6 copy-start.9
  10.6 0.7 slice-start
  13.1 6.7 %copy-start.7 = (s32[2,8,4]{1,2,0:T(4,128)S(1)}, s32[2,8,4]{1,2,0:T(4,128)}, u32[]{:S(2)}) copy-start(s32[2,8,4]{1,2,0:T(4,128)} %param.7) | copy-start | bytes 772
  13.1 6.8 %copy-start.8 = (s32[2,8,4]{1,2,0:T(4,128)S(1)}, s32[2,8,4]{1,2,0:T(4,128)}, u32[]{:S(2)}) copy-start(s32[2,8,4]{1,2,0:T(4,128)} %param.8) | copy-start | bytes 772
  13.1 7.6 %copy-start.10 = (f32[256]{0:T(256)S(1)}, f32[256]{0:T(256)}, u32[]{:S(2)}) copy-start(f32[256]{0:T(256)} %copy-done.9) | copy-start | bytes 3076
  13.2 7.7 %copy-start.3 = (f32[1,2,8,128,128]{4,3,2,1,0:T(8,128)S(1)}, f32[1,2,8,128,128]{4,3,2,1,0:T(8,128)}, u32[]{:S(2)}) copy-start(f32[1,2,8,128,128]{4,3,2,1,0:T(8,128)} %param.6) | copy-start | bytes 3145732
  16.7 1.9 %copy-start.1 = (f32[16,128,512]{2,1,0:T(8,128)}, f32[16,128,512]{2,1,0:T(8,128)S(1)}, u32[]{:S(2)}) copy-start(f32[16,128,512]{2,1,0:T(8,128)S(1)} %convolution_bitcast_fusion.1) | copy-start | bytes 12582916
  30.1 2.0 %copy-start.2 = (f32[16,128,512]{2,1,0:T(8,128)}, f32[16,128,512]{2,1,0:T(8,128)S(1)}, u32[]{:S(2)}) copy-start(f32[16,128,512]{2,1,0:T(8,128)S(1)} %convolution_bitcast_fusion) | copy-start | bytes 12582916
  49.9 10.8 %collective-permute-start.2 = (f32[1,64,1024]{1,2,0:T(8,128)}, f32[1,64,1024]{1,2,0:T(8,128)}, u32[]{:S(2)}, u32[]{:S(2)}) collective-permute-start(f32[1,64,1024]{1,2,0:T(8,128)} %slice_bitcast_fusion.11), channel_id=1, source_target_pairs={{0,1},{1,2},{2,3},{3,4},{4,5},{5,6},{6,7},{8,9},{9,10},{10,11},{11... | collective-permute-start | bytes 786440 | tf_op jit(solution)/shard_map/ppermute | solution.py:32
  53.0 10.6 %collective-permute-start.3 = (f32[1,64,1024]{1,2,0:T(8,128)}, f32[1,64,1024]{1,2,0:T(8,128)}, u32[]{:S(2)}, u32[]{:S(2)}) collective-permute-start(f32[1,64,1024]{1,2,0:T(8,128)} %slice_bitcast_fusion.8), channel_id=1, source_target_pairs={{1,0},{2,1},{3,2},{4,3},{5,4},{6,5},{7,6},{9,8},{10,9},{11,10},{12... | collective-permute-start | bytes 786440 | tf_op jit(solution)/shard_map/ppermute | solution.py:32
  57.4 1.1 %copy-start.4 = (f32[8,192,128]{2,1,0:T(8,128)S(1)}, f32[8,192,128]{2,1,0:T(8,128)}, u32[]{:S(2)}) copy-start(f32[8,192,128]{2,1,0:T(8,128)} %get-tuple-element.44) | copy-start | bytes 2359300
  57.4 1.4 %copy-start.5 = (f32[8,192,128]{2,1,0:T(8,128)S(1)}, f32[8,192,128]{2,1,0:T(8,128)}, u32[]{:S(2)}) copy-start(f32[8,192,128]{2,1,0:T(8,128)} %get-tuple-element.46) | copy-start | bytes 2359300
